TPU v7x, 32 devices: a whole 2x2x4 slice. The times are simulated.
32 devices in a mesh: parts: 2 (over x), chain: 16 (over z, y, core).
Axes of the slice: x: 2, y: 2, z: 4, core: 2. Of those that a mesh axis runs over, the one named last changes fastest.
Arguments:
- subspace: float32 [64, 8192], P('parts', 'chain'), parts along dimension 0, may hold values from -4 to 4
- s_inv: float32 [8, 32, 2, 256, 256], P('parts', 'chain'), parts along dimension 0, may hold values from -1 to 1
- couple: float32 [32, 512, 256], P('chain', 'parts'), parts along dimension 1, may hold values from -1 to 1
- diag_blocks: float32 [32, 512, 256], P('chain', 'parts'), parts along dimension 1, may hold values from -4 to 4
- weights: float32 [8, 2], P('parts'), parts along dimension 0, may hold values from -1 to 1
Outputs:
- filtered: float32 [64, 8192], P('parts', 'chain'), parts along dimension 0
- applied: float32 [64, 8192], P('parts', 'chain'), parts along dimension 0
- grams: float32 [2, 64, 32], P(None, 'parts'), parts along dimension 1
There are 2 independent parts, one for each index of `parts`. A program takes and returns all parts, laid end to end along the dimension named above; each array names one. Nothing has to cross between parts.
All inputs are finite; a program needn't handle non-finite values.
Results may differ from a plain program's by a relative error of at most 0.00027.
Values sent between devices are 32-bit elements; how exact they have to be, the bound alone decides.
No kernel may reach another device: no remote copies, remote signals or barrier semaphores. Data moves between devices by JAX's collectives and lax.ppermute only.
A program may use at most 192 MiB of HBM per device.

v0:
```python
import jax
import jax.numpy as jnp
from jax import lax
from jax.sharding import PartitionSpec as P

highest = lax.Precision.HIGHEST


def passed_along(shard, axis, by):
    peers = lax.axis_size(axis)
    pairs = [(i, i + by) for i in range(peers) if 0 <= i + by < peers]
    return lax.ppermute(shard, axis, pairs)


def inverse_apply(pivot_inv, vecs):
    real_part = jnp.einsum(
        "qnk,qjk->qnj", vecs[:, 0], pivot_inv[:, 0], precision=highest
    ) - jnp.einsum("qnk,qjk->qnj", vecs[:, 1], pivot_inv[:, 1], precision=highest)
    imag_part = jnp.einsum(
        "qnk,qjk->qnj", vecs[:, 0], pivot_inv[:, 1], precision=highest
    ) + jnp.einsum("qnk,qjk->qnj", vecs[:, 1], pivot_inv[:, 0], precision=highest)
    return jnp.stack([real_part, imag_part], axis=1)


def right_apply(vecs, matrix):
    real_part = jnp.einsum(
        "qnk,qkj->qnj", vecs[:, 0], matrix[:, 0], precision=highest
    ) - jnp.einsum("qnk,qkj->qnj", vecs[:, 1], matrix[:, 1], precision=highest)
    imag_part = jnp.einsum(
        "qnk,qkj->qnj", vecs[:, 0], matrix[:, 1], precision=highest
    ) + jnp.einsum("qnk,qkj->qnj", vecs[:, 1], matrix[:, 0], precision=highest)
    return jnp.stack([real_part, imag_part], axis=1)


def couple_down(coupling_blk, vecs):
    return jnp.einsum("qcnk,kj->qcnj", vecs, coupling_blk, precision=highest)


def couple_up(coupling_blk, vecs):
    return jnp.einsum("qcnk,jk->qcnj", vecs, coupling_blk, precision=highest)


def sweep_forward(pivots, couple, start_rows, source, store_all):
    blocks_dev = couple.shape[0]

    def advance(carried, position):
        pivot_inv = lax.dynamic_index_in_dim(pivots, position, 1, keepdims=False)
        coupling_blk = lax.dynamic_index_in_dim(couple, position, 0, keepdims=False)
        combined = carried
        if source is not None:
            rhs_block = lax.dynamic_index_in_dim(source, position, 0, keepdims=False)
            combined = combined.at[:, 0].add(rhs_block[None])
        solved = inverse_apply(pivot_inv, combined)
        return (couple_down(coupling_blk, solved), solved if store_all else None)

    return lax.scan(advance, start_rows, jnp.arange(blocks_dev))


def sweep_backward(pivots, couple, start_rows, solved_all, store_all):
    blocks_dev = couple.shape[0]

    def retreat(carried, position):
        pivot_inv = lax.dynamic_index_in_dim(pivots, position, 1, keepdims=False)
        coupling_blk = lax.dynamic_index_in_dim(couple, position, 0, keepdims=False)
        correction = inverse_apply(pivot_inv, couple_up(coupling_blk, carried))
        if solved_all is not None:
            correction = (
                lax.dynamic_index_in_dim(solved_all, position, 0, keepdims=False) + correction
            )
        return (correction, correction if store_all else None)

    return lax.scan(retreat, start_rows, jnp.arange(blocks_dev), reverse=True)


def shards(subspace, s_inv, couple, diag_blocks, weights):
    points = s_inv.shape[0]
    blocks_dev = couple.shape[0]
    block_width = couple.shape[1]
    vectors = subspace.shape[0]
    source = subspace.reshape(vectors, blocks_dev, block_width).transpose(1, 0, 2)
    zero_rows = jnp.zeros((points, 2, vectors, block_width), jnp.float32)
    plain_eye = jnp.stack(
        [
            jnp.eye(block_width, dtype=jnp.float32),
            jnp.zeros((block_width, block_width), jnp.float32),
        ]
    )
    identity_map = jnp.broadcast_to(plain_eye, (points, 2, block_width, block_width))
    chain_size = lax.axis_size("chain")
    forward_map, _ = sweep_forward(s_inv, couple, identity_map, None, False)
    forward_tip, _ = sweep_forward(s_inv, couple, zero_rows, source, False)

    def forward_hop(hop_index, inbound):
        return passed_along(right_apply(inbound, forward_map) + forward_tip, "chain", 1)

    incoming = lax.fori_loop(0, chain_size - 1, forward_hop, zero_rows)
    _, solved_all = sweep_forward(s_inv, couple, incoming, source, True)
    backward_map, _ = sweep_backward(s_inv, couple, identity_map, None, False)
    backward_tip, _ = sweep_backward(s_inv, couple, zero_rows, solved_all, False)

    def backward_hop(hop_index, inbound):
        return passed_along(right_apply(inbound, backward_map) + backward_tip, "chain", -1)

    outgoing = lax.fori_loop(0, chain_size - 1, backward_hop, zero_rows)
    _, result = sweep_backward(s_inv, couple, outgoing, solved_all, True)
    signed = weights * jnp.array([1.0, -1.0], jnp.float32)
    filtered_blocks = jnp.einsum("rqcnk,qc->rnk", result, signed, precision=highest)
    down_all = jnp.einsum("rnk,rkj->rnj", filtered_blocks, couple, precision=highest)
    from_next = passed_along(filtered_blocks[0], "chain", -1)
    from_prior = passed_along(down_all[-1], "chain", 1)
    diag_term = jnp.einsum("rnk,rjk->rnj", filtered_blocks, diag_blocks, precision=highest)
    upper_rows = jnp.concatenate([filtered_blocks[1:], from_next[None]], axis=0)
    term_up = jnp.einsum("rnk,rjk->rnj", upper_rows, couple, precision=highest)
    lower_rows = jnp.concatenate([from_prior[None], down_all[:-1]], axis=0)
    applied_blocks = diag_term + term_up + lower_rows
    gram_plain = jnp.einsum("rnk,rmk->nm", filtered_blocks, filtered_blocks, precision=highest)
    gram_matrix = jnp.einsum("rnk,rmk->nm", filtered_blocks, applied_blocks, precision=highest)
    summed = lax.psum(jnp.stack([gram_plain, gram_matrix]), "chain")
    grams = summed / (blocks_dev * block_width * chain_size)
    filtered = filtered_blocks.transpose(1, 0, 2).reshape(vectors, blocks_dev * block_width)
    applied = applied_blocks.transpose(1, 0, 2).reshape(vectors, blocks_dev * block_width)
    return (filtered, applied, grams)


def solution(mesh):
    placed = (
        P("parts", "chain"),
        P("parts", "chain", None, None, None),
        P("chain", "parts", None),
        P("chain", "parts", None),
        P("parts", None),
    )
    return jax.shard_map(
        shards,
        mesh=mesh,
        in_specs=placed,
        out_specs=(P("parts", "chain"), P("parts", "chain"), P(None, "parts", None)),
        check_vma=False,
    )
```

profile of v0, /device:TPU:0, one launch (start us, length us, event | category | flops | bytes accessed | tf_op | source)
XLA Modules:
  0.0 591.9 jit_solution(1425416484922783797)
XLA Ops:
  0.7 4.6 copy.49
  6.5 25.1 %while.104 = (s32[]{:T(128)}, f32[4,2,256,256]{3,2,1,0:T(8,128)S(1)}, s32[2]{0:T(128)S(1)}, f32[4,2,2,256,256]{4,3,0,2,1:T(8,128)}, f32[2,256,256]{2,1,0:T(8,128)S(1)}, /*index=5*/s32[]{:T(128)}, s32[]{:T(128)}, s32[]{:T(128)}) while((s32[]{:T(128)}, f32[4,2,256,256]{3,2,1,0:T(8,128)S(1)}, s32[2]{0:T(128)S(1)}, ...), condition=%wide.region_3.4_spmd, body=%wide.region_2.3_spmd.sunk | while | flops 4832886784 | bytes 23330956 | solution.py:56
  15.4 3.6 fusion.219
  28.0 3.6 fusion.219
  33.3 18.5 %while.105 = (s32[]{:T(128)}, f32[4,2,32,256]{3,2,1,0:T(8,128)S(1)}, s32[2]{0:T(128)S(1)}, f32[2,32,256]{2,1,0:T(8,128)S(1)}, f32[4,2,2,256,256]{4,3,0,2,1:T(8,1...) while((s32[]{:T(128)}, f32[4,2,32,256]{3,2,1,0:T(8,128)S(1)}, s32[2]{0:T(128)S(1)}, ...), condition=%wide.region_5.6_spmd, body=%wide.region_4.5_spmd.sunk | while | flops 604176384 | bytes 10616983 | solution.py:56
  52.6 173.2 %while.106 = (s32[]{:T(128)}, f32[4,2,32,256]{3,2,0,1:T(8,128)S(1)}, f32[4,2,256,256]{3,2,0,1:T(8,128)S(1)}, f32[4,2,32,256]{3,2,0,1:T(8,128)}, s32[]{:T(128)}) while((s32[]{:T(128)}, f32[4,2,32,256]{3,2,0,1:T(8,128)S(1)}, f32[4,2,256,256]{3,2,0,1:T(8,128)S(1)}, f32[4,2,32,256]{3,2,0,1:T(8,128)}, s32[]{:T(128)}) %tuple.236), condition=%wide.region_7.8_spmd, body=%wide.region_6.7_spmd.sunk | while | flops 402849792 | bytes 8388737 | solution.py:96
  56.2 2.4 collective-permute-start
  63.6 6.8 %collective-permute-start = (f32[4,2,32,256]{3,2,0,1:T(8,128)}, f32[4,2,32,256]{3,2,0,1:T(8,128)S(1)}, u32[]{:S(2)}, u32[]{:S(2)}) collective-permute-start(f32[4,2,32,256]{3,2,0,1:T(8,128)} %maximum_add_fusion.10), channel_id=1, source_target_pairs={{0,1},{1,2},{2,3},{3,4},{4,5},{5,6},{6,7},{7,8},{8,9},{9,10},{10,1... | collective-permute-start | bytes 786440 | tf_op jit(solution)/shard_map/while/body/eval_jaxpr/ppermute | solution.py:12
  75.3 6.5 %collective-permute-start = (f32[4,2,32,256]{3,2,0,1:T(8,128)}, f32[4,2,32,256]{3,2,0,1:T(8,128)S(1)}, u32[]{:S(2)}, u32[]{:S(2)}) collective-permute-start(f32[4,2,32,256]{3,2,0,1:T(8,128)} %maximum_add_fusion.10), channel_id=1, source_target_pairs={{0,1},{1,2},{2,3},{3,4},{4,5},{5,6},{6,7},{7,8},{8,9},{9,10},{10,1... | collective-permute-start | bytes 786440 | tf_op jit(solution)/shard_map/while/body/eval_jaxpr/ppermute | solution.py:12
  86.8 6.5 %collective-permute-start = (f32[4,2,32,256]{3,2,0,1:T(8,128)}, f32[4,2,32,256]{3,2,0,1:T(8,128)S(1)}, u32[]{:S(2)}, u32[]{:S(2)}) collective-permute-start(f32[4,2,32,256]{3,2,0,1:T(8,128)} %maximum_add_fusion.10), channel_id=1, source_target_pairs={{0,1},{1,2},{2,3},{3,4},{4,5},{5,6},{6,7},{7,8},{8,9},{9,10},{10,1... | collective-permute-start | bytes 786440 | tf_op jit(solution)/shard_map/while/body/eval_jaxpr/ppermute | solution.py:12
  98.3 6.5 %collective-permute-start = (f32[4,2,32,256]{3,2,0,1:T(8,128)}, f32[4,2,32,256]{3,2,0,1:T(8,128)S(1)}, u32[]{:S(2)}, u32[]{:S(2)}) collective-permute-start(f32[4,2,32,256]{3,2,0,1:T(8,128)} %maximum_add_fusion.10), channel_id=1, source_target_pairs={{0,1},{1,2},{2,3},{3,4},{4,5},{5,6},{6,7},{7,8},{8,9},{9,10},{10,1... | collective-permute-start | bytes 786440 | tf_op jit(solution)/shard_map/while/body/eval_jaxpr/ppermute | solution.py:12
  109.8 6.5 %collective-permute-start = (f32[4,2,32,256]{3,2,0,1:T(8,128)}, f32[4,2,32,256]{3,2,0,1:T(8,128)S(1)}, u32[]{:S(2)}, u32[]{:S(2)}) collective-permute-start(f32[4,2,32,256]{3,2,0,1:T(8,128)} %maximum_add_fusion.10), channel_id=1, source_target_pairs={{0,1},{1,2},{2,3},{3,4},{4,5},{5,6},{6,7},{7,8},{8,9},{9,10},{10,1... | collective-permute-start | bytes 786440 | tf_op jit(solution)/shard_map/while/body/eval_jaxpr/ppermute | solution.py:12
  121.3 6.5 %collective-permute-start = (f32[4,2,32,256]{3,2,0,1:T(8,128)}, f32[4,2,32,256]{3,2,0,1:T(8,128)S(1)}, u32[]{:S(2)}, u32[]{:S(2)}) collective-permute-start(f32[4,2,32,256]{3,2,0,1:T(8,128)} %maximum_add_fusion.10), channel_id=1, source_target_pairs={{0,1},{1,2},{2,3},{3,4},{4,5},{5,6},{6,7},{7,8},{8,9},{9,10},{10,1... | collective-permute-start | bytes 786440 | tf_op jit(solution)/shard_map/while/body/eval_jaxpr/ppermute | solution.py:12
  132.8 6.5 %collective-permute-start = (f32[4,2,32,256]{3,2,0,1:T(8,128)}, f32[4,2,32,256]{3,2,0,1:T(8,128)S(1)}, u32[]{:S(2)}, u32[]{:S(2)}) collective-permute-start(f32[4,2,32,256]{3,2,0,1:T(8,128)} %maximum_add_fusion.10), channel_id=1, source_target_pairs={{0,1},{1,2},{2,3},{3,4},{4,5},{5,6},{6,7},{7,8},{8,9},{9,10},{10,1... | collective-permute-start | bytes 786440 | tf_op jit(solution)/shard_map/while/body/eval_jaxpr/ppermute | solution.py:12
  144.3 6.5 %collective-permute-start = (f32[4,2,32,256]{3,2,0,1:T(8,128)}, f32[4,2,32,256]{3,2,0,1:T(8,128)S(1)}, u32[]{:S(2)}, u32[]{:S(2)}) collective-permute-start(f32[4,2,32,256]{3,2,0,1:T(8,128)} %maximum_add_fusion.10), channel_id=1, source_target_pairs={{0,1},{1,2},{2,3},{3,4},{4,5},{5,6},{6,7},{7,8},{8,9},{9,10},{10,1... | collective-permute-start | bytes 786440 | tf_op jit(solution)/shard_map/while/body/eval_jaxpr/ppermute | solution.py:12
  155.9 6.6 %collective-permute-start = (f32[4,2,32,256]{3,2,0,1:T(8,128)}, f32[4,2,32,256]{3,2,0,1:T(8,128)S(1)}, u32[]{:S(2)}, u32[]{:S(2)}) collective-permute-start(f32[4,2,32,256]{3,2,0,1:T(8,128)} %maximum_add_fusion.10), channel_id=1, source_target_pairs={{0,1},{1,2},{2,3},{3,4},{4,5},{5,6},{6,7},{7,8},{8,9},{9,10},{10,1... | collective-permute-start | bytes 786440 | tf_op jit(solution)/shard_map/while/body/eval_jaxpr/ppermute | solution.py:12
  167.4 7.4 %collective-permute-start = (f32[4,2,32,256]{3,2,0,1:T(8,128)}, f32[4,2,32,256]{3,2,0,1:T(8,128)S(1)}, u32[]{:S(2)}, u32[]{:S(2)}) collective-permute-start(f32[4,2,32,256]{3,2,0,1:T(8,128)} %maximum_add_fusion.10), channel_id=1, source_target_pairs={{0,1},{1,2},{2,3},{3,4},{4,5},{5,6},{6,7},{7,8},{8,9},{9,10},{10,1... | collective-permute-start | bytes 786440 | tf_op jit(solution)/shard_map/while/body/eval_jaxpr/ppermute | solution.py:12
  179.8 7.4 %collective-permute-start = (f32[4,2,32,256]{3,2,0,1:T(8,128)}, f32[4,2,32,256]{3,2,0,1:T(8,128)S(1)}, u32[]{:S(2)}, u32[]{:S(2)}) collective-permute-start(f32[4,2,32,256]{3,2,0,1:T(8,128)} %maximum_add_fusion.10), channel_id=1, source_target_pairs={{0,1},{1,2},{2,3},{3,4},{4,5},{5,6},{6,7},{7,8},{8,9},{9,10},{10,1... | collective-permute-start | bytes 786440 | tf_op jit(solution)/shard_map/while/body/eval_jaxpr/ppermute | solution.py:12
  192.2 7.4 %collective-permute-start = (f32[4,2,32,256]{3,2,0,1:T(8,128)}, f32[4,2,32,256]{3,2,0,1:T(8,128)S(1)}, u32[]{:S(2)}, u32[]{:S(2)}) collective-permute-start(f32[4,2,32,256]{3,2,0,1:T(8,128)} %maximum_add_fusion.10), channel_id=1, source_target_pairs={{0,1},{1,2},{2,3},{3,4},{4,5},{5,6},{6,7},{7,8},{8,9},{9,10},{10,1... | collective-permute-start | bytes 786440 | tf_op jit(solution)/shard_map/while/body/eval_jaxpr/ppermute | solution.py:12
  204.6 7.4 %collective-permute-start = (f32[4,2,32,256]{3,2,0,1:T(8,128)}, f32[4,2,32,256]{3,2,0,1:T(8,128)S(1)}, u32[]{:S(2)}, u32[]{:S(2)}) collective-permute-start(f32[4,2,32,256]{3,2,0,1:T(8,128)} %maximum_add_fusion.10), channel_id=1, source_target_pairs={{0,1},{1,2},{2,3},{3,4},{4,5},{5,6},{6,7},{7,8},{8,9},{9,10},{10,1... | collective-permute-start | bytes 786440 | tf_op jit(solution)/shard_map/while/body/eval_jaxpr/ppermute | solution.py:12
  217.0 7.4 %collective-permute-start = (f32[4,2,32,256]{3,2,0,1:T(8,128)}, f32[4,2,32,256]{3,2,0,1:T(8,128)S(1)}, u32[]{:S(2)}, u32[]{:S(2)}) collective-permute-start(f32[4,2,32,256]{3,2,0,1:T(8,128)} %maximum_add_fusion.10), channel_id=1, source_target_pairs={{0,1},{1,2},{2,3},{3,4},{4,5},{5,6},{6,7},{7,8},{8,9},{9,10},{10,1... | collective-permute-start | bytes 786440 | tf_op jit(solution)/shard_map/while/body/eval_jaxpr/ppermute | solution.py:12
  225.8 18.2 %while.107 = (s32[]{:T(128)}, f32[4,2,32,256]{3,2,1,0:T(8,128)S(1)}, f32[2,4,2,32,256]{4,3,1,2,0:T(8,128)}, s32[2]{0:T(128)S(1)}, f32[2,32,256]{2,1,0:T(8,128)S(...) while((s32[]{:T(128)}, f32[4,2,32,256]{3,2,1,0:T(8,128)S(1)}, ...), condition=%wide.region_9.10_spmd, body=%wide.region_8.9_spmd.sunk | while | flops 604241920 | bytes 15335643 | solution.py:56
  244.0 19.8 %while.110 = (s32[]{:T(128)}, f32[4,2,32,256]{3,2,0,1:T(8,128)}, s32[2]{0:T(128)S(1)}, f32[2,4,2,32,256]{4,3,1,2,0:T(8,128)}, f32[2,256,256]{2,1,0:T(8,128)S(1)}...) while((s32[]{:T(128)}, f32[4,2,32,256]{3,2,0,1:T(8,128)}, ...), condition=%wide.region_11.12_spmd.clone, body=%wide.region_10.11_spmd.clone.sunk | while | flops 604241920 | bytes 13369545 | solution.py:72
  265.1 27.5 %while.103 = (s32[]{:T(128)}, f32[4,2,256,256]{3,2,0,1:T(8,128)S(1)}, s32[2]{0:T(128)S(1)}, f32[2,256,256]{2,1,0:T(8,128)S(1)}, f32[4,2,2,256,256]{4,3,0,2,1:T(8,128)}, /*index=5*/s32[]{:T(128)}, s32[]{:T(128)}, s32[]{:T(128)}) while((s32[]{:T(128)}, f32[4,2,256,256]{3,2,0,1:T(8,128)S(1)}, s32[2]{0:T(128)S(1)}, f32[2,256,256]{2,1,0:T(8,128)S(1)}, ...), condition=%wide.region_1.2_spmd, body=%wide.region_0.1_spmd.sunk | while | flops 4832886784 | bytes 27525272 | solution.py:72
  269.1 1.9 fusion.204
  271.0 1.9 fusion.207
  273.0 1.9 fusion.208
  282.9 1.9 fusion.204
  286.7 1.9 fusion.208
  292.6 201.3 %while.108 = (s32[]{:T(128)}, f32[4,2,32,256]{3,2,0,1:T(8,128)S(1)}, f32[4,2,256,256]{3,2,0,1:T(8,128)S(1)}, f32[4,2,32,256]{3,2,0,1:T(8,128)}, s32[]{:T(128)}) while((s32[]{:T(128)}, f32[4,2,32,256]{3,2,0,1:T(8,128)S(1)}, f32[4,2,256,256]{3,2,0,1:T(8,128)S(1)}, f32[4,2,32,256]{3,2,0,1:T(8,128)}, s32[]{:T(128)}) %tuple.225), condition=%wide.region_13.14_spmd, body=%wide.region_12.13_spmd.sunk | while | flops 402849792 | bytes 7340133 | solution.py:104
  298.7 7.4 %collective-permute-done.1 = f32[4,2,32,256]{3,2,0,1:T(8,128)S(1)} collective-permute-done((f32[4,2,32,256]{3,2,0,1:T(8,128)}, f32[4,2,32,256]{3,2,0,1:T(8,128)S(1)}, u32[]{:S(2)}, u32[]{:S(2)}) %collective-permute-start.1) | collective-permute-done | bytes 262176 | tf_op jit(solution)/shard_map/while/body/eval_jaxpr/ppermute | solution.py:12
  311.9 8.1 %collective-permute-done.1 = f32[4,2,32,256]{3,2,0,1:T(8,128)S(1)} collective-permute-done((f32[4,2,32,256]{3,2,0,1:T(8,128)}, f32[4,2,32,256]{3,2,0,1:T(8,128)S(1)}, u32[]{:S(2)}, u32[]{:S(2)}) %collective-permute-start.1) | collective-permute-done | bytes 262176 | tf_op jit(solution)/shard_map/while/body/eval_jaxpr/ppermute | solution.py:12
  325.9 7.4 %collective-permute-done.1 = f32[4,2,32,256]{3,2,0,1:T(8,128)S(1)} collective-permute-done((f32[4,2,32,256]{3,2,0,1:T(8,128)}, f32[4,2,32,256]{3,2,0,1:T(8,128)S(1)}, u32[]{:S(2)}, u32[]{:S(2)}) %collective-permute-start.1) | collective-permute-done | bytes 262176 | tf_op jit(solution)/shard_map/while/body/eval_jaxpr/ppermute | solution.py:12
  339.1 8.1 %collective-permute-done.1 = f32[4,2,32,256]{3,2,0,1:T(8,128)S(1)} collective-permute-done((f32[4,2,32,256]{3,2,0,1:T(8,128)}, f32[4,2,32,256]{3,2,0,1:T(8,128)S(1)}, u32[]{:S(2)}, u32[]{:S(2)}) %collective-permute-start.1) | collective-permute-done | bytes 262176 | tf_op jit(solution)/shard_map/while/body/eval_jaxpr/ppermute | solution.py:12
  353.1 7.5 %collective-permute-done.1 = f32[4,2,32,256]{3,2,0,1:T(8,128)S(1)} collective-permute-done((f32[4,2,32,256]{3,2,0,1:T(8,128)}, f32[4,2,32,256]{3,2,0,1:T(8,128)S(1)}, u32[]{:S(2)}, u32[]{:S(2)}) %collective-permute-start.1) | collective-permute-done | bytes 262176 | tf_op jit(solution)/shard_map/while/body/eval_jaxpr/ppermute | solution.py:12
  366.4 7.5 %collective-permute-done.1 = f32[4,2,32,256]{3,2,0,1:T(8,128)S(1)} collective-permute-done((f32[4,2,32,256]{3,2,0,1:T(8,128)}, f32[4,2,32,256]{3,2,0,1:T(8,128)S(1)}, u32[]{:S(2)}, u32[]{:S(2)}) %collective-permute-start.1) | collective-permute-done | bytes 262176 | tf_op jit(solution)/shard_map/while/body/eval_jaxpr/ppermute | solution.py:12
  379.8 7.5 %collective-permute-done.1 = f32[4,2,32,256]{3,2,0,1:T(8,128)S(1)} collective-permute-done((f32[4,2,32,256]{3,2,0,1:T(8,128)}, f32[4,2,32,256]{3,2,0,1:T(8,128)S(1)}, u32[]{:S(2)}, u32[]{:S(2)}) %collective-permute-start.1) | collective-permute-done | bytes 262176 | tf_op jit(solution)/shard_map/while/body/eval_jaxpr/ppermute | solution.py:12
  393.1 7.5 %collective-permute-done.1 = f32[4,2,32,256]{3,2,0,1:T(8,128)S(1)} collective-permute-done((f32[4,2,32,256]{3,2,0,1:T(8,128)}, f32[4,2,32,256]{3,2,0,1:T(8,128)S(1)}, u32[]{:S(2)}, u32[]{:S(2)}) %collective-permute-start.1) | collective-permute-done | bytes 262176 | tf_op jit(solution)/shard_map/while/body/eval_jaxpr/ppermute | solution.py:12
  406.4 7.5 %collective-permute-done.1 = f32[4,2,32,256]{3,2,0,1:T(8,128)S(1)} collective-permute-done((f32[4,2,32,256]{3,2,0,1:T(8,128)}, f32[4,2,32,256]{3,2,0,1:T(8,128)S(1)}, u32[]{:S(2)}, u32[]{:S(2)}) %collective-permute-start.1) | collective-permute-done | bytes 262176 | tf_op jit(solution)/shard_map/while/body/eval_jaxpr/ppermute | solution.py:12
  419.8 7.5 %collective-permute-done.1 = f32[4,2,32,256]{3,2,0,1:T(8,128)S(1)} collective-permute-done((f32[4,2,32,256]{3,2,0,1:T(8,128)}, f32[4,2,32,256]{3,2,0,1:T(8,128)S(1)}, u32[]{:S(2)}, u32[]{:S(2)}) %collective-permute-start.1) | collective-permute-done | bytes 262176 | tf_op jit(solution)/shard_map/while/body/eval_jaxpr/ppermute | solution.py:12
  433.1 7.5 %collective-permute-done.1 = f32[4,2,32,256]{3,2,0,1:T(8,128)S(1)} collective-permute-done((f32[4,2,32,256]{3,2,0,1:T(8,128)}, f32[4,2,32,256]{3,2,0,1:T(8,128)S(1)}, u32[]{:S(2)}, u32[]{:S(2)}) %collective-permute-start.1) | collective-permute-done | bytes 262176 | tf_op jit(solution)/shard_map/while/body/eval_jaxpr/ppermute | solution.py:12
  446.4 7.5 %collective-permute-done.1 = f32[4,2,32,256]{3,2,0,1:T(8,128)S(1)} collective-permute-done((f32[4,2,32,256]{3,2,0,1:T(8,128)}, f32[4,2,32,256]{3,2,0,1:T(8,128)S(1)}, u32[]{:S(2)}, u32[]{:S(2)}) %collective-permute-start.1) | collective-permute-done | bytes 262176 | tf_op jit(solution)/shard_map/while/body/eval_jaxpr/ppermute | solution.py:12
  459.8 7.5 %collective-permute-done.1 = f32[4,2,32,256]{3,2,0,1:T(8,128)S(1)} collective-permute-done((f32[4,2,32,256]{3,2,0,1:T(8,128)}, f32[4,2,32,256]{3,2,0,1:T(8,128)S(1)}, u32[]{:S(2)}, u32[]{:S(2)}) %collective-permute-start.1) | collective-permute-done | bytes 262176 | tf_op jit(solution)/shard_map/while/body/eval_jaxpr/ppermute | solution.py:12
  473.1 7.5 %collective-permute-done.1 = f32[4,2,32,256]{3,2,0,1:T(8,128)S(1)} collective-permute-done((f32[4,2,32,256]{3,2,0,1:T(8,128)}, f32[4,2,32,256]{3,2,0,1:T(8,128)S(1)}, u32[]{:S(2)}, u32[]{:S(2)}) %collective-permute-start.1) | collective-permute-done | bytes 262176 | tf_op jit(solution)/shard_map/while/body/eval_jaxpr/ppermute | solution.py:12
  486.5 7.5 %collective-permute-done.1 = f32[4,2,32,256]{3,2,0,1:T(8,128)S(1)} collective-permute-done((f32[4,2,32,256]{3,2,0,1:T(8,128)}, f32[4,2,32,256]{3,2,0,1:T(8,128)S(1)}, u32[]{:S(2)}, u32[]{:S(2)}) %collective-permute-start.1) | collective-permute-done | bytes 262176 | tf_op jit(solution)/shard_map/while/body/eval_jaxpr/ppermute | solution.py:12
  494.1 18.5 %while.109 = (s32[]{:T(128)}, f32[4,2,32,256]{3,2,0,1:T(8,128)S(1)}, f32[2,4,2,32,256]{4,1,2,3,0:T(4,128)S(1)}, s32[2]{0:T(128)S(1)}, f32[2,4,2,32,256]{4,3,1,2,...) while((s32[]{:T(128)}, f32[4,2,32,256]{3,2,0,1:T(8,128)S(1)}, ...), condition=%wide.region_15.16_spmd, body=%wide.region_14.15_spmd.sunk | while | flops 604307456 | bytes 14680271 | solution.py:72
  515.1 8.2 %collective-permute-start.3 = (f32[32,256]{1,0:T(8,128)S(1)}, f32[32,256]{1,0:T(8,128)S(1)}, u32[]{:S(2)}, u32[]{:S(2)}) collective-permute-start(f32[32,256]{1,0:T(8,128)S(1)} %get-tuple-element.827), channel_id=1, source_target_pairs={{0,1},{1,2},{2,3},{3,4},{4,5},{5,6},{6,7},{7,8},{8,9},{9,10},{10,1... | collective-permute-start | bytes 98312 | tf_op jit(solution)/shard_map/ppermute | solution.py:12
  525.5 64.7 %psum.7 = f32[2,32,32]{2,1,0:T(8,128)S(1)} all-reduce(f32[2,32,32]{2,1,0:T(8,128)S(1)} %pad_maximum_fusion.4), channel_id=1, replica_groups=mesh['parts'=2,'chain'=16] {'chain'}, use_global_device_ids=true, to_apply=%region_16.17 | all-reduce | flops 2048 | bytes 16384 | tf_op jit(solution)/shard_map/psum | solution.py:118
  (371 shorter events, 258.9 us)
Async XLA Ops:
  0.6 522.6 %copy-start = (f32[2,256,256]{2,1,0:T(8,128)S(1)}, f32[2,256,256]{2,1,0:T(8,128)}, u32[]{:S(2)}) copy-start(f32[2,256,256]{2,1,0:T(8,128)} %param.29) | copy-start | bytes 1572868
  33.3 19.3 %copy-start.1 = (f32[4,2,256,256]{3,2,0,1:T(8,128)S(1)}, f32[4,2,256,256]{3,2,0,1:T(8,128)}, u32[]{:S(2)}) copy-start(f32[4,2,256,256]{3,2,0,1:T(8,128)} %copy.54) | copy-start | bytes 6291460
  56.2 3.7 collective-permute-start
  63.6 8.1 %collective-permute-start = (f32[4,2,32,256]{3,2,0,1:T(8,128)}, f32[4,2,32,256]{3,2,0,1:T(8,128)S(1)}, u32[]{:S(2)}, u32[]{:S(2)}) collective-permute-start(f32[4,2,32,256]{3,2,0,1:T(8,128)} %maximum_add_fusion.10), channel_id=1, source_target_pairs={{0,1},{1,2},{2,3},{3,4},{4,5},{5,6},{6,7},{7,8},{8,9},{9,10},{10,1... | collective-permute-start | bytes 786440 | tf_op jit(solution)/shard_map/while/body/eval_jaxpr/ppermute | solution.py:12
  75.3 7.9 %collective-permute-start = (f32[4,2,32,256]{3,2,0,1:T(8,128)}, f32[4,2,32,256]{3,2,0,1:T(8,128)S(1)}, u32[]{:S(2)}, u32[]{:S(2)}) collective-permute-start(f32[4,2,32,256]{3,2,0,1:T(8,128)} %maximum_add_fusion.10), channel_id=1, source_target_pairs={{0,1},{1,2},{2,3},{3,4},{4,5},{5,6},{6,7},{7,8},{8,9},{9,10},{10,1... | collective-permute-start | bytes 786440 | tf_op jit(solution)/shard_map/while/body/eval_jaxpr/ppermute | solution.py:12
  86.8 7.9 %collective-permute-start = (f32[4,2,32,256]{3,2,0,1:T(8,128)}, f32[4,2,32,256]{3,2,0,1:T(8,128)S(1)}, u32[]{:S(2)}, u32[]{:S(2)}) collective-permute-start(f32[4,2,32,256]{3,2,0,1:T(8,128)} %maximum_add_fusion.10), channel_id=1, source_target_pairs={{0,1},{1,2},{2,3},{3,4},{4,5},{5,6},{6,7},{7,8},{8,9},{9,10},{10,1... | collective-permute-start | bytes 786440 | tf_op jit(solution)/shard_map/while/body/eval_jaxpr/ppermute | solution.py:12
  98.3 7.9 %collective-permute-start = (f32[4,2,32,256]{3,2,0,1:T(8,128)}, f32[4,2,32,256]{3,2,0,1:T(8,128)S(1)}, u32[]{:S(2)}, u32[]{:S(2)}) collective-permute-start(f32[4,2,32,256]{3,2,0,1:T(8,128)} %maximum_add_fusion.10), channel_id=1, source_target_pairs={{0,1},{1,2},{2,3},{3,4},{4,5},{5,6},{6,7},{7,8},{8,9},{9,10},{10,1... | collective-permute-start | bytes 786440 | tf_op jit(solution)/shard_map/while/body/eval_jaxpr/ppermute | solution.py:12
  106.9 2.1 copy-start.7
  109.8 7.9 %collective-permute-start = (f32[4,2,32,256]{3,2,0,1:T(8,128)}, f32[4,2,32,256]{3,2,0,1:T(8,128)S(1)}, u32[]{:S(2)}, u32[]{:S(2)}) collective-permute-start(f32[4,2,32,256]{3,2,0,1:T(8,128)} %maximum_add_fusion.10), channel_id=1, source_target_pairs={{0,1},{1,2},{2,3},{3,4},{4,5},{5,6},{6,7},{7,8},{8,9},{9,10},{10,1... | collective-permute-start | bytes 786440 | tf_op jit(solution)/shard_map/while/body/eval_jaxpr/ppermute | solution.py:12
  118.4 2.1 copy-start.7
  121.3 7.9 %collective-permute-start = (f32[4,2,32,256]{3,2,0,1:T(8,128)}, f32[4,2,32,256]{3,2,0,1:T(8,128)S(1)}, u32[]{:S(2)}, u32[]{:S(2)}) collective-permute-start(f32[4,2,32,256]{3,2,0,1:T(8,128)} %maximum_add_fusion.10), channel_id=1, source_target_pairs={{0,1},{1,2},{2,3},{3,4},{4,5},{5,6},{6,7},{7,8},{8,9},{9,10},{10,1... | collective-permute-start | bytes 786440 | tf_op jit(solution)/shard_map/while/body/eval_jaxpr/ppermute | solution.py:12
  129.9 2.1 copy-start.7
  132.8 7.9 %collective-permute-start = (f32[4,2,32,256]{3,2,0,1:T(8,128)}, f32[4,2,32,256]{3,2,0,1:T(8,128)S(1)}, u32[]{:S(2)}, u32[]{:S(2)}) collective-permute-start(f32[4,2,32,256]{3,2,0,1:T(8,128)} %maximum_add_fusion.10), channel_id=1, source_target_pairs={{0,1},{1,2},{2,3},{3,4},{4,5},{5,6},{6,7},{7,8},{8,9},{9,10},{10,1... | collective-permute-start | bytes 786440 | tf_op jit(solution)/shard_map/while/body/eval_jaxpr/ppermute | solution.py:12
  141.4 2.1 copy-start.7
  144.3 7.9 %collective-permute-start = (f32[4,2,32,256]{3,2,0,1:T(8,128)}, f32[4,2,32,256]{3,2,0,1:T(8,128)S(1)}, u32[]{:S(2)}, u32[]{:S(2)}) collective-permute-start(f32[4,2,32,256]{3,2,0,1:T(8,128)} %maximum_add_fusion.10), channel_id=1, source_target_pairs={{0,1},{1,2},{2,3},{3,4},{4,5},{5,6},{6,7},{7,8},{8,9},{9,10},{10,1... | collective-permute-start | bytes 786440 | tf_op jit(solution)/shard_map/while/body/eval_jaxpr/ppermute | solution.py:12
  155.9 7.9 %collective-permute-start = (f32[4,2,32,256]{3,2,0,1:T(8,128)}, f32[4,2,32,256]{3,2,0,1:T(8,128)S(1)}, u32[]{:S(2)}, u32[]{:S(2)}) collective-permute-start(f32[4,2,32,256]{3,2,0,1:T(8,128)} %maximum_add_fusion.10), channel_id=1, source_target_pairs={{0,1},{1,2},{2,3},{3,4},{4,5},{5,6},{6,7},{7,8},{8,9},{9,10},{10,1... | collective-permute-start | bytes 786440 | tf_op jit(solution)/shard_map/while/body/eval_jaxpr/ppermute | solution.py:12
  164.5 2.1 copy-start.7
  167.4 8.8 %collective-permute-start = (f32[4,2,32,256]{3,2,0,1:T(8,128)}, f32[4,2,32,256]{3,2,0,1:T(8,128)S(1)}, u32[]{:S(2)}, u32[]{:S(2)}) collective-permute-start(f32[4,2,32,256]{3,2,0,1:T(8,128)} %maximum_add_fusion.10), channel_id=1, source_target_pairs={{0,1},{1,2},{2,3},{3,4},{4,5},{5,6},{6,7},{7,8},{8,9},{9,10},{10,1... | collective-permute-start | bytes 786440 | tf_op jit(solution)/shard_map/while/body/eval_jaxpr/ppermute | solution.py:12
  179.8 8.8 %collective-permute-start = (f32[4,2,32,256]{3,2,0,1:T(8,128)}, f32[4,2,32,256]{3,2,0,1:T(8,128)S(1)}, u32[]{:S(2)}, u32[]{:S(2)}) collective-permute-start(f32[4,2,32,256]{3,2,0,1:T(8,128)} %maximum_add_fusion.10), channel_id=1, source_target_pairs={{0,1},{1,2},{2,3},{3,4},{4,5},{5,6},{6,7},{7,8},{8,9},{9,10},{10,1... | collective-permute-start | bytes 786440 | tf_op jit(solution)/shard_map/while/body/eval_jaxpr/ppermute | solution.py:12
  189.3 2.1 copy-start.7
  192.2 8.8 %collective-permute-start = (f32[4,2,32,256]{3,2,0,1:T(8,128)}, f32[4,2,32,256]{3,2,0,1:T(8,128)S(1)}, u32[]{:S(2)}, u32[]{:S(2)}) collective-permute-start(f32[4,2,32,256]{3,2,0,1:T(8,128)} %maximum_add_fusion.10), channel_id=1, source_target_pairs={{0,1},{1,2},{2,3},{3,4},{4,5},{5,6},{6,7},{7,8},{8,9},{9,10},{10,1... | collective-permute-start | bytes 786440 | tf_op jit(solution)/shard_map/while/body/eval_jaxpr/ppermute | solution.py:12
  204.6 8.8 %collective-permute-start = (f32[4,2,32,256]{3,2,0,1:T(8,128)}, f32[4,2,32,256]{3,2,0,1:T(8,128)S(1)}, u32[]{:S(2)}, u32[]{:S(2)}) collective-permute-start(f32[4,2,32,256]{3,2,0,1:T(8,128)} %maximum_add_fusion.10), channel_id=1, source_target_pairs={{0,1},{1,2},{2,3},{3,4},{4,5},{5,6},{6,7},{7,8},{8,9},{9,10},{10,1... | collective-permute-start | bytes 786440 | tf_op jit(solution)/shard_map/while/body/eval_jaxpr/ppermute | solution.py:12
  217.0 8.8 %collective-permute-start = (f32[4,2,32,256]{3,2,0,1:T(8,128)}, f32[4,2,32,256]{3,2,0,1:T(8,128)S(1)}, u32[]{:S(2)}, u32[]{:S(2)}) collective-permute-start(f32[4,2,32,256]{3,2,0,1:T(8,128)} %maximum_add_fusion.10), channel_id=1, source_target_pairs={{0,1},{1,2},{2,3},{3,4},{4,5},{5,6},{6,7},{7,8},{8,9},{9,10},{10,1... | collective-permute-start | bytes 786440 | tf_op jit(solution)/shard_map/while/body/eval_jaxpr/ppermute | solution.py:12
  230.9 3.2 copy-start.3
  239.9 3.2 copy-start.3
  249.6 3.2 copy-start.5
  259.9 3.2 copy-start.5
  297.4 8.7 %collective-permute-start.1 = (f32[4,2,32,256]{3,2,0,1:T(8,128)}, f32[4,2,32,256]{3,2,0,1:T(8,128)S(1)}, u32[]{:S(2)}, u32[]{:S(2)}) collective-permute-start(f32[4,2,32,256]{3,2,0,1:T(8,128)} %maximum_add_fusion.11), channel_id=1, source_target_pairs={{1,0},{2,1},{3,2},{4,3},{5,4},{6,5},{7,6},{8,7},{9,8},{10,9},{11,1... | collective-permute-start | bytes 786440 | tf_op jit(solution)/shard_map/while/body/eval_jaxpr/ppermute | solution.py:12
  310.7 9.4 %collective-permute-start.1 = (f32[4,2,32,256]{3,2,0,1:T(8,128)}, f32[4,2,32,256]{3,2,0,1:T(8,128)S(1)}, u32[]{:S(2)}, u32[]{:S(2)}) collective-permute-start(f32[4,2,32,256]{3,2,0,1:T(8,128)} %maximum_add_fusion.11), channel_id=1, source_target_pairs={{1,0},{2,1},{3,2},{4,3},{5,4},{6,5},{7,6},{8,7},{9,8},{10,9},{11,1... | collective-permute-start | bytes 786440 | tf_op jit(solution)/shard_map/while/body/eval_jaxpr/ppermute | solution.py:12
  324.6 8.7 %collective-permute-start.1 = (f32[4,2,32,256]{3,2,0,1:T(8,128)}, f32[4,2,32,256]{3,2,0,1:T(8,128)S(1)}, u32[]{:S(2)}, u32[]{:S(2)}) collective-permute-start(f32[4,2,32,256]{3,2,0,1:T(8,128)} %maximum_add_fusion.11), channel_id=1, source_target_pairs={{1,0},{2,1},{3,2},{4,3},{5,4},{6,5},{7,6},{8,7},{9,8},{10,9},{11,1... | collective-permute-start | bytes 786440 | tf_op jit(solution)/shard_map/while/body/eval_jaxpr/ppermute | solution.py:12
  337.8 9.4 %collective-permute-start.1 = (f32[4,2,32,256]{3,2,0,1:T(8,128)}, f32[4,2,32,256]{3,2,0,1:T(8,128)S(1)}, u32[]{:S(2)}, u32[]{:S(2)}) collective-permute-start(f32[4,2,32,256]{3,2,0,1:T(8,128)} %maximum_add_fusion.11), channel_id=1, source_target_pairs={{1,0},{2,1},{3,2},{4,3},{5,4},{6,5},{7,6},{8,7},{9,8},{10,9},{11,1... | collective-permute-start | bytes 786440 | tf_op jit(solution)/shard_map/while/body/eval_jaxpr/ppermute | solution.py:12
  351.8 8.8 %collective-permute-start.1 = (f32[4,2,32,256]{3,2,0,1:T(8,128)}, f32[4,2,32,256]{3,2,0,1:T(8,128)S(1)}, u32[]{:S(2)}, u32[]{:S(2)}) collective-permute-start(f32[4,2,32,256]{3,2,0,1:T(8,128)} %maximum_add_fusion.11), channel_id=1, source_target_pairs={{1,0},{2,1},{3,2},{4,3},{5,4},{6,5},{7,6},{8,7},{9,8},{10,9},{11,1... | collective-permute-start | bytes 786440 | tf_op jit(solution)/shard_map/while/body/eval_jaxpr/ppermute | solution.py:12
  365.1 8.8 %collective-permute-start.1 = (f32[4,2,32,256]{3,2,0,1:T(8,128)}, f32[4,2,32,256]{3,2,0,1:T(8,128)S(1)}, u32[]{:S(2)}, u32[]{:S(2)}) collective-permute-start(f32[4,2,32,256]{3,2,0,1:T(8,128)} %maximum_add_fusion.11), channel_id=1, source_target_pairs={{1,0},{2,1},{3,2},{4,3},{5,4},{6,5},{7,6},{8,7},{9,8},{10,9},{11,1... | collective-permute-start | bytes 786440 | tf_op jit(solution)/shard_map/while/body/eval_jaxpr/ppermute | solution.py:12
  378.5 8.8 %collective-permute-start.1 = (f32[4,2,32,256]{3,2,0,1:T(8,128)}, f32[4,2,32,256]{3,2,0,1:T(8,128)S(1)}, u32[]{:S(2)}, u32[]{:S(2)}) collective-permute-start(f32[4,2,32,256]{3,2,0,1:T(8,128)} %maximum_add_fusion.11), channel_id=1, source_target_pairs={{1,0},{2,1},{3,2},{4,3},{5,4},{6,5},{7,6},{8,7},{9,8},{10,9},{11,1... | collective-permute-start | bytes 786440 | tf_op jit(solution)/shard_map/while/body/eval_jaxpr/ppermute | solution.py:12
  391.8 8.8 %collective-permute-start.1 = (f32[4,2,32,256]{3,2,0,1:T(8,128)}, f32[4,2,32,256]{3,2,0,1:T(8,128)S(1)}, u32[]{:S(2)}, u32[]{:S(2)}) collective-permute-start(f32[4,2,32,256]{3,2,0,1:T(8,128)} %maximum_add_fusion.11), channel_id=1, source_target_pairs={{1,0},{2,1},{3,2},{4,3},{5,4},{6,5},{7,6},{8,7},{9,8},{10,9},{11,1... | collective-permute-start | bytes 786440 | tf_op jit(solution)/shard_map/while/body/eval_jaxpr/ppermute | solution.py:12
  405.2 8.8 %collective-permute-start.1 = (f32[4,2,32,256]{3,2,0,1:T(8,128)}, f32[4,2,32,256]{3,2,0,1:T(8,128)S(1)}, u32[]{:S(2)}, u32[]{:S(2)}) collective-permute-start(f32[4,2,32,256]{3,2,0,1:T(8,128)} %maximum_add_fusion.11), channel_id=1, source_target_pairs={{1,0},{2,1},{3,2},{4,3},{5,4},{6,5},{7,6},{8,7},{9,8},{10,9},{11,1... | collective-permute-start | bytes 786440 | tf_op jit(solution)/shard_map/while/body/eval_jaxpr/ppermute | solution.py:12
  418.5 8.8 %collective-permute-start.1 = (f32[4,2,32,256]{3,2,0,1:T(8,128)}, f32[4,2,32,256]{3,2,0,1:T(8,128)S(1)}, u32[]{:S(2)}, u32[]{:S(2)}) collective-permute-start(f32[4,2,32,256]{3,2,0,1:T(8,128)} %maximum_add_fusion.11), channel_id=1, source_target_pairs={{1,0},{2,1},{3,2},{4,3},{5,4},{6,5},{7,6},{8,7},{9,8},{10,9},{11,1... | collective-permute-start | bytes 786440 | tf_op jit(solution)/shard_map/while/body/eval_jaxpr/ppermute | solution.py:12
  431.8 8.8 %collective-permute-start.1 = (f32[4,2,32,256]{3,2,0,1:T(8,128)}, f32[4,2,32,256]{3,2,0,1:T(8,128)S(1)}, u32[]{:S(2)}, u32[]{:S(2)}) collective-permute-start(f32[4,2,32,256]{3,2,0,1:T(8,128)} %maximum_add_fusion.11), channel_id=1, source_target_pairs={{1,0},{2,1},{3,2},{4,3},{5,4},{6,5},{7,6},{8,7},{9,8},{10,9},{11,1... | collective-permute-start | bytes 786440 | tf_op jit(solution)/shard_map/while/body/eval_jaxpr/ppermute | solution.py:12
  445.2 8.8 %collective-permute-start.1 = (f32[4,2,32,256]{3,2,0,1:T(8,128)}, f32[4,2,32,256]{3,2,0,1:T(8,128)S(1)}, u32[]{:S(2)}, u32[]{:S(2)}) collective-permute-start(f32[4,2,32,256]{3,2,0,1:T(8,128)} %maximum_add_fusion.11), channel_id=1, source_target_pairs={{1,0},{2,1},{3,2},{4,3},{5,4},{6,5},{7,6},{8,7},{9,8},{10,9},{11,1... | collective-permute-start | bytes 786440 | tf_op jit(solution)/shard_map/while/body/eval_jaxpr/ppermute | solution.py:12
  458.5 8.8 %collective-permute-start.1 = (f32[4,2,32,256]{3,2,0,1:T(8,128)}, f32[4,2,32,256]{3,2,0,1:T(8,128)S(1)}, u32[]{:S(2)}, u32[]{:S(2)}) collective-permute-start(f32[4,2,32,256]{3,2,0,1:T(8,128)} %maximum_add_fusion.11), channel_id=1, source_target_pairs={{1,0},{2,1},{3,2},{4,3},{5,4},{6,5},{7,6},{8,7},{9,8},{10,9},{11,1... | collective-permute-start | bytes 786440 | tf_op jit(solution)/shard_map/while/body/eval_jaxpr/ppermute | solution.py:12
  471.8 8.8 %collective-permute-start.1 = (f32[4,2,32,256]{3,2,0,1:T(8,128)}, f32[4,2,32,256]{3,2,0,1:T(8,128)S(1)}, u32[]{:S(2)}, u32[]{:S(2)}) collective-permute-start(f32[4,2,32,256]{3,2,0,1:T(8,128)} %maximum_add_fusion.11), channel_id=1, source_target_pairs={{1,0},{2,1},{3,2},{4,3},{5,4},{6,5},{7,6},{8,7},{9,8},{10,9},{11,1... | collective-permute-start | bytes 786440 | tf_op jit(solution)/shard_map/while/body/eval_jaxpr/ppermute | solution.py:12
  485.2 8.8 %collective-permute-start.1 = (f32[4,2,32,256]{3,2,0,1:T(8,128)}, f32[4,2,32,256]{3,2,0,1:T(8,128)S(1)}, u32[]{:S(2)}, u32[]{:S(2)}) collective-permute-start(f32[4,2,32,256]{3,2,0,1:T(8,128)} %maximum_add_fusion.11), channel_id=1, source_target_pairs={{1,0},{2,1},{3,2},{4,3},{5,4},{6,5},{7,6},{8,7},{9,8},{10,9},{11,1... | collective-permute-start | bytes 786440 | tf_op jit(solution)/shard_map/while/body/eval_jaxpr/ppermute | solution.py:12
  494.0 18.5 %copy-start.10 = (f32[4,2]{0,1:T(2,128)S(1)}, f32[4,2]{0,1:T(2,128)}, u32[]{:S(2)}) copy-start(f32[4,2]{0,1:T(2,128)} %param.30) | copy-start | bytes 100
  494.0 18.5 %copy-start.11 = (f32[2]{0:T(128)S(1)}, f32[2]{0:T(128)}, u32[]{:S(2)}) copy-start(f32[2]{0:T(128)} %constant.277.clone) | copy-start | bytes 28
  499.8 3.2 copy-start.6
  509.1 3.2 copy-start.6
  513.3 11.3 %collective-permute-start.2 = (f32[32,256]{1,0:T(8,128)S(1)}, f32[32,256]{1,0:T(8,128)S(1)}, u32[]{:S(2)}, u32[]{:S(2)}) collective-permute-start(f32[32,256]{1,0:T(8,128)S(1)} %get-tuple-element.830), channel_id=1, source_target_pairs={{1,0},{2,1},{3,2},{4,3},{5,4},{6,5},{7,6},{8,7},{9,8},{10,9},{11,1... | collective-permute-start | bytes 98312 | tf_op jit(solution)/shard_map/ppermute | solution.py:12
  515.1 9.6 %collective-permute-start.3 = (f32[32,256]{1,0:T(8,128)S(1)}, f32[32,256]{1,0:T(8,128)S(1)}, u32[]{:S(2)}, u32[]{:S(2)}) collective-permute-start(f32[32,256]{1,0:T(8,128)S(1)} %get-tuple-element.827), channel_id=1, source_target_pairs={{0,1},{1,2},{2,3},{3,4},{4,5},{5,6},{6,7},{7,8},{8,9},{9,10},{10,1... | collective-permute-start | bytes 98312 | tf_op jit(solution)/shard_map/ppermute | solution.py:12
  (14 other events, 24.5 us)
where the time goes:
time: 601 us; the launch traced here: 592 us
  matrix products  161 us (27%)
  waiting for transfers between devices  134 us (22%)
  starting transfers between devices  127 us (21%)
  blocking collectives  64.7 us (11%)
  local copies, waits for them, and re-layouts  39.9 us (7%)
  other arithmetic  39.4 us (7%)
  loops' own time  24.9 us (4%)
    ppermute x32, waiting for transfers between devices, passed_along(): return lax.ppermute(shard, axis, pairs)  134 us
    ppermute x32, starting transfers between devices, passed_along(): return lax.ppermute(shard, axis, pairs)  127 us
    psum x1, blocking collectives, shards(): summed = lax.psum(jnp.stack([gram_plain, gram_matrix]), 'chain')  64.7 us
    add x15, other arithmetic, backward_hop(): right_apply(inbound, backward_map) + backward_tip  25.5 us
    dot_general x30, matrix products, right_apply(): jnp.einsum('qnk,qkj->qnj', vecs[:, 1], matrix[:, 0], precision=highest)  21.1 us
    dot_general x30, matrix products, right_apply(): jnp.einsum('qnk,qkj->qnj', vecs[:, 1], matrix[:, 1], precision=highest)  21.1 us
    dot_general x30, matrix products, right_apply(): jnp.einsum('qnk,qkj->qnj', vecs[:, 0], matrix[:, 0], precision=highest)  21.1 us
    dot_general x30, matrix products, right_apply(): jnp.einsum('qnk,qkj->qnj', vecs[:, 0], matrix[:, 1], precision=highest)  21.1 us
  transfers between devices with their start and end apart: 32, of which 30 were waited for; matrix products, arithmetic and copies ran while one was open for 0% of the time, Pallas kernels for 0%

commit v1 on v0

--- a/solution.py
+++ b/solution.py
@@ -12,6 +12,17 @@
     return lax.ppermute(shard, axis, pairs)
 
 
+def chain_sum(value, axis):
+    peers = lax.axis_size(axis)
+    if peers & (peers - 1):
+        return lax.psum(value, axis)
+    stride = 1
+    while stride < peers:
+        value = value + lax.ppermute(value, axis, [(i, i ^ stride) for i in range(peers)])
+        stride *= 2
+    return value
+
+
 def inverse_apply(pivot_inv, vecs):
     real_part = jnp.einsum(
         "qnk,qjk->qnj", vecs[:, 0], pivot_inv[:, 0], precision=highest
@@ -19,16 +30,6 @@
     imag_part = jnp.einsum(
         "qnk,qjk->qnj", vecs[:, 0], pivot_inv[:, 1], precision=highest
     ) + jnp.einsum("qnk,qjk->qnj", vecs[:, 1], pivot_inv[:, 0], precision=highest)
-    return jnp.stack([real_part, imag_part], axis=1)
-
-
-def right_apply(vecs, matrix):
-    real_part = jnp.einsum(
-        "qnk,qkj->qnj", vecs[:, 0], matrix[:, 0], precision=highest
-    ) - jnp.einsum("qnk,qkj->qnj", vecs[:, 1], matrix[:, 1], precision=highest)
-    imag_part = jnp.einsum(
-        "qnk,qkj->qnj", vecs[:, 0], matrix[:, 1], precision=highest
-    ) + jnp.einsum("qnk,qkj->qnj", vecs[:, 1], matrix[:, 0], precision=highest)
     return jnp.stack([real_part, imag_part], axis=1)
 
 
@@ -40,7 +41,7 @@
     return jnp.einsum("qcnk,jk->qcnj", vecs, coupling_blk, precision=highest)
 
 
-def sweep_forward(pivots, couple, start_rows, source, store_all):
+def sweep_forward(pivots, couple, start_rows, source, rhs_rows, store_all):
     blocks_dev = couple.shape[0]
 
     def advance(carried, position):
@@ -49,14 +50,14 @@
         combined = carried
         if source is not None:
             rhs_block = lax.dynamic_index_in_dim(source, position, 0, keepdims=False)
-            combined = combined.at[:, 0].add(rhs_block[None])
+            combined = combined.at[:, 0, rhs_rows:].add(rhs_block[None])
         solved = inverse_apply(pivot_inv, combined)
         return (couple_down(coupling_blk, solved), solved if store_all else None)
 
     return lax.scan(advance, start_rows, jnp.arange(blocks_dev))
 
 
-def sweep_backward(pivots, couple, start_rows, solved_all, store_all):
+def sweep_backward(pivots, couple, start_rows, solved_all, rhs_rows, store_all):
     blocks_dev = couple.shape[0]
 
     def retreat(carried, position):
@@ -64,12 +65,47 @@
         coupling_blk = lax.dynamic_index_in_dim(couple, position, 0, keepdims=False)
         correction = inverse_apply(pivot_inv, couple_up(coupling_blk, carried))
         if solved_all is not None:
-            correction = (
-                lax.dynamic_index_in_dim(solved_all, position, 0, keepdims=False) + correction
-            )
+            known = lax.dynamic_index_in_dim(solved_all, position, 0, keepdims=False)
+            correction = correction.at[:, :, rhs_rows:].add(known)
         return (correction, correction if store_all else None)
 
     return lax.scan(retreat, start_rows, jnp.arange(blocks_dev), reverse=True)
+
+
+def block_real(matrix):
+    top = jnp.concatenate([matrix[:, 0], matrix[:, 1]], axis=2)
+    bottom = jnp.concatenate([-matrix[:, 1], matrix[:, 0]], axis=2)
+    return jnp.concatenate([top, bottom], axis=1)
+
+
+def flat_rows(vecs):
+    return jnp.concatenate([vecs[:, 0], vecs[:, 1]], axis=2)
+
+
+def unflat_rows(flat, width):
+    return jnp.stack([flat[..., :width], flat[..., width:]], axis=1)
+
+
+def pipelined_chain(maps, tips, by):
+    points = tips.shape[0]
+    peers = lax.axis_size("chain")
+    rank = lax.axis_index("chain")
+    depth = rank if by > 0 else peers - 1 - rank
+
+    def step(stage, inbox):
+        point = jnp.clip(stage - depth, 0, points - 1)
+        rows = lax.dynamic_index_in_dim(inbox, point, 0, keepdims=False)
+        out = jnp.dot(
+            rows, lax.dynamic_index_in_dim(maps, point, 0, keepdims=False), precision=highest
+        ) + lax.dynamic_index_in_dim(tips, point, 0, keepdims=False)
+        got = passed_along(out, "chain", by)
+        slot = stage + 1 - depth
+        keep = (slot >= 0) & (slot < points)
+        slot = jnp.clip(slot, 0, points - 1)
+        current = lax.dynamic_index_in_dim(inbox, slot, 0, keepdims=False)
+        return lax.dynamic_update_index_in_dim(inbox, jnp.where(keep, got, current), slot, 0)
+
+    return lax.fori_loop(0, peers + points - 2, step, jnp.zeros_like(tips))
 
 
 def shards(subspace, s_inv, couple, diag_blocks, weights):
@@ -87,22 +123,23 @@
     )
     identity_map = jnp.broadcast_to(plain_eye, (points, 2, block_width, block_width))
     chain_size = lax.axis_size("chain")
-    forward_map, _ = sweep_forward(s_inv, couple, identity_map, None, False)
-    forward_tip, _ = sweep_forward(s_inv, couple, zero_rows, source, False)
 
-    def forward_hop(hop_index, inbound):
-        return passed_along(right_apply(inbound, forward_map) + forward_tip, "chain", 1)
+    forward_start = jnp.concatenate([identity_map, zero_rows], axis=2)
+    forward_both, _ = sweep_forward(s_inv, couple, forward_start, source, block_width, False)
+    forward_map = forward_both[:, :, :block_width]
+    forward_tip = forward_both[:, :, block_width:]
+    incoming = unflat_rows(
+        pipelined_chain(block_real(forward_map), flat_rows(forward_tip), 1), block_width
+    )
+    _, solved_all = sweep_forward(s_inv, couple, incoming, source, 0, True)
 
-    incoming = lax.fori_loop(0, chain_size - 1, forward_hop, zero_rows)
-    _, solved_all = sweep_forward(s_inv, couple, incoming, source, True)
-    backward_map, _ = sweep_backward(s_inv, couple, identity_map, None, False)
-    backward_tip, _ = sweep_backward(s_inv, couple, zero_rows, solved_all, False)
+    backward_map, _ = sweep_backward(s_inv, couple, identity_map, None, 0, False)
+    backward_tip, _ = sweep_backward(s_inv, couple, zero_rows, solved_all, 0, False)
+    outgoing = unflat_rows(
+        pipelined_chain(block_real(backward_map), flat_rows(backward_tip), -1), block_width
+    )
+    _, result = sweep_backward(s_inv, couple, outgoing, solved_all, 0, True)
 
-    def backward_hop(hop_index, inbound):
-        return passed_along(right_apply(inbound, backward_map) + backward_tip, "chain", -1)
-
-    outgoing = lax.fori_loop(0, chain_size - 1, backward_hop, zero_rows)
-    _, result = sweep_backward(s_inv, couple, outgoing, solved_all, True)
     signed = weights * jnp.array([1.0, -1.0], jnp.float32)
     filtered_blocks = jnp.einsum("rqcnk,qc->rnk", result, signed, precision=highest)
     down_all = jnp.einsum("rnk,rkj->rnj", filtered_blocks, couple, precision=highest)
@@ -115,7 +152,7 @@
     applied_blocks = diag_term + term_up + lower_rows
     gram_plain = jnp.einsum("rnk,rmk->nm", filtered_blocks, filtered_blocks, precision=highest)
     gram_matrix = jnp.einsum("rnk,rmk->nm", filtered_blocks, applied_blocks, precision=highest)
-    summed = lax.psum(jnp.stack([gram_plain, gram_matrix]), "chain")
+    summed = chain_sum(jnp.stack([gram_plain, gram_matrix]), "chain")
     grams = summed / (blocks_dev * block_width * chain_size)
     filtered = filtered_blocks.transpose(1, 0, 2).reshape(vectors, blocks_dev * block_width)
     applied = applied_blocks.transpose(1, 0, 2).reshape(vectors, blocks_dev * block_width)

time: 601 us -> 480 us (0.80)
  blocking collectives: 64.7 us -> 0 us
  matrix products: 161 us -> 133 us
  waiting for transfers between devices: 134 us -> 114 us
  other arithmetic: 39.4 us -> 19.5 us
  starting transfers between devices: 127 us -> 139 us
  local copies, waits for them, and re-layouts: 39.9 us -> 46 us
    psum x1 -> x0, blocking collectives: 64.7 us -> none  [shards(): summed = lax.psum(jnp.stack([gram_plain, gram_matrix]), 'chain')]
    add x36 -> x9, other arithmetic: 38.3 us -> 0.28 us  [the longest x6 0.25 us: retreat(): correction = correction.at[:, :, rhs_rows:].add(known)]
    ppermute x32 -> x38, waiting for transfers between devices: 134 us -> 109 us  [passed_along(): return lax.ppermute(shard, axis, pairs)]
    ppermute x0 -> x4, starting transfers between devices: none -> 16.3 us  [chain_sum(): lax.ppermute(value, axis, [(i, i ^ stride) for i in range(peers)])]
    dot_general x120 -> x36, matrix products: 84.4 us -> 69.6 us  [step(): jnp.dot(rows, lax.dynamic_index_in_dim(maps, point, 0, keepdims=False), p...]
    concatenate x0 -> x4, other arithmetic: none -> 10.3 us  [the longest x2 9.29 us: block_real(): return jnp.concatenate([top, bottom], axis=1)]
    ppermute x32 -> x38, starting transfers between devices: 127 us -> 122 us  [passed_along(): return lax.ppermute(shard, axis, pairs)]
    dot_general x12 -> x10, matrix products: 14.6 us -> 12.7 us  [inverse_apply(): jnp.einsum('qnk,qjk->qnj', vecs[:, 1], pivot_inv[:, 0], precision=highest)]
  transfers between devices with their start and end apart: 32 -> 42, of which waited for: 30 -> 41; matrix products, arithmetic and copies ran while one was open for 0% -> 1% of each run, Pallas kernels for 0% -> 0%
where the time goes in v1:
time: 480 us; the launch traced here: 477 us
  starting transfers between devices  139 us (29%)
  matrix products  133 us (28%)
  waiting for transfers between devices  114 us (24%)
  local copies, waits for them, and re-layouts  46 us (10%)
  loops' own time  23.9 us (5%)
  other arithmetic  19.5 us (4%)
    ppermute x38, starting transfers between devices, passed_along(): return lax.ppermute(shard, axis, pairs)  122 us
    ppermute x38, waiting for transfers between devices, passed_along(): return lax.ppermute(shard, axis, pairs)  109 us
    dot_general x36, matrix products, step(): jnp.dot(rows, lax.dynamic_index_in_dim(maps, point, 0, keepdims=False), p...  69.6 us
    ppermute x4, starting transfers between devices, chain_sum(): lax.ppermute(value, axis, [(i, i ^ stride) for i in range(peers)])  16.3 us
    another operation x3, loops' own time, sweep_backward(): return lax.scan(retreat, start_rows, jnp.arange(blocks_dev), reverse=True)  12.8 us
    dot_general x10, matrix products, inverse_apply(): jnp.einsum('qnk,qjk->qnj', vecs[:, 1], pivot_inv[:, 1], precision=highest)  12.7 us
    dot_general x10, matrix products, inverse_apply(): jnp.einsum('qnk,qjk->qnj', vecs[:, 1], pivot_inv[:, 0], precision=highest)  12.7 us
    dot_general x10, matrix products, inverse_apply(): jnp.einsum('qnk,qjk->qnj', vecs[:, 0], pivot_inv[:, 0], precision=highest)  12.6 us
  transfers between devices with their start and end apart: 42, of which 41 were waited for; matrix products, arithmetic and copies ran while one was open for 1% of the time, Pallas kernels for 0%

profile of v1, /device:TPU:0, one launch (start us, length us, event | category | flops | bytes accessed | tf_op | source)
XLA Modules:
  0.0 476.5 jit_solution(3725679848134838153)
XLA Ops:
  0.7 4.6 copy.44
  7.4 36.6 %while.104 = (s32[]{:T(128)}, f32[4,2,288,256]{3,2,1,0:T(8,128)S(1)}, s32[2]{0:T(128)S(1)}, f32[2,32,256]{2,1,0:T(8,128)S(1)}, f32[4,2,2,256,256]{4,3,0,2,1:T(8,...) while((s32[]{:T(128)}, ...), condition=%wide.region_4.5_spmd, body=%wide.region_2.4_spmd.sunk | while | flops 5437063168 | bytes 40468796 | solution.py:57
  48.7 28.2 %while.103 = (s32[]{:T(128)}, f32[4,2,256,256]{3,2,0,1:T(8,128)S(1)}, s32[2]{0:T(128)S(1)}, f32[2,256,256]{2,1,0:T(8,128)S(1)}, f32[4,2,2,256,256]{4,3,0,2,1:T(8,128)}, /*index=5*/s32[]{:T(128)}, s32[]{:T(128)}, s32[]{:T(128)}) while((s32[]{:T(128)}, f32[4,2,256,256]{3,2,0,1:T(8,128)S(1)}, s32[2]{0:T(128)S(1)}, f32[2,256,256]{2,1,0:T(8,128)S(1)}, ...), condition=%wide.region_1.2_spmd, body=%wide.region_0.1_spmd.sunk | while | flops 4832886784 | bytes 27525272 | solution.py:72
  80.6 4.8 %maximum_maximum_fusion.1 = f32[4,512,512]{2,1,0:T(8,128)} fusion(f32[4,256,256]{2,1,0:T(8,128)} %get-tuple-element.973, f32[4,256,256]{2,1,0:T(8,128)} %fusion.69, f32[4,256,256]{2,1,0:T(8,128)} %get-tuple-element.972), kind=kLoop, calls=%fused_computation.118 | loop fusion | flops 3145728 | bytes 7340032 | tf_op jit(solution)/shard_map/concatenate | solution.py:78
  85.4 143.2 %while.105 = (s32[]{:T(128)}, f32[4,32,512]{2,1,0:T(8,128)S(1)}, s32[]{:T(128)}, f32[4,512,512]{2,1,0:T(8,128)}, f32[4,32,512]{2,1,0:T(8,128)S(1)}, /*index=5*/s32[]{:T(128)}, s32[]{:T(128)}, s32[]{:T(128)}, s32[]{:T(128)}) while((s32[]{:T(128)}, f32[4,32,512]{2,1,0:T(8,128)S(1)}, s32[]{:T(128)}, f32[4,512,512]{2,1,0:T(8,128)}, ...), condition=%wide.region_6.7_spmd, body=%wide.region_5.6_spmd.sunk | while | flops 100696072 | bytes 1836779 | solution.py:108
  92.7 5.0 %collective-permute-start = (f32[32,512]{1,0:T(8,128)S(1)}, f32[32,512]{1,0:T(8,128)S(1)}, u32[]{:S(2)}, u32[]{:S(2)}) collective-permute-start(f32[32,512]{1,0:T(8,128)S(1)} %convolution_add_fusion.10), channel_id=1, source_target_pairs={{0,1},{1,2},{2,3},{3,4},{4,5},{5,6},{6,7},{7,8},{8,9},{9,10},{10,1... | collective-permute-start | bytes 196616 | tf_op jit(solution)/shard_map/while/body/eval_jaxpr/ppermute | solution.py:12
  100.5 4.7 collective-permute-start
  108.0 4.7 collective-permute-start
  115.6 4.7 collective-permute-start
  123.2 4.7 collective-permute-start
  130.7 4.7 collective-permute-start
  138.3 4.8 %collective-permute-start = (f32[32,512]{1,0:T(8,128)S(1)}, f32[32,512]{1,0:T(8,128)S(1)}, u32[]{:S(2)}, u32[]{:S(2)}) collective-permute-start(f32[32,512]{1,0:T(8,128)S(1)} %convolution_add_fusion.10), channel_id=1, source_target_pairs={{0,1},{1,2},{2,3},{3,4},{4,5},{5,6},{6,7},{7,8},{8,9},{9,10},{10,1... | collective-permute-start | bytes 196616 | tf_op jit(solution)/shard_map/while/body/eval_jaxpr/ppermute | solution.py:12
  145.9 5.6 %collective-permute-start = (f32[32,512]{1,0:T(8,128)S(1)}, f32[32,512]{1,0:T(8,128)S(1)}, u32[]{:S(2)}, u32[]{:S(2)}) collective-permute-start(f32[32,512]{1,0:T(8,128)S(1)} %convolution_add_fusion.10), channel_id=1, source_target_pairs={{0,1},{1,2},{2,3},{3,4},{4,5},{5,6},{6,7},{7,8},{8,9},{9,10},{10,1... | collective-permute-start | bytes 196616 | tf_op jit(solution)/shard_map/while/body/eval_jaxpr/ppermute | solution.py:12
  154.4 5.6 %collective-permute-start = (f32[32,512]{1,0:T(8,128)S(1)}, f32[32,512]{1,0:T(8,128)S(1)}, u32[]{:S(2)}, u32[]{:S(2)}) collective-permute-start(f32[32,512]{1,0:T(8,128)S(1)} %convolution_add_fusion.10), channel_id=1, source_target_pairs={{0,1},{1,2},{2,3},{3,4},{4,5},{5,6},{6,7},{7,8},{8,9},{9,10},{10,1... | collective-permute-start | bytes 196616 | tf_op jit(solution)/shard_map/while/body/eval_jaxpr/ppermute | solution.py:12
  162.8 5.6 %collective-permute-start = (f32[32,512]{1,0:T(8,128)S(1)}, f32[32,512]{1,0:T(8,128)S(1)}, u32[]{:S(2)}, u32[]{:S(2)}) collective-permute-start(f32[32,512]{1,0:T(8,128)S(1)} %convolution_add_fusion.10), channel_id=1, source_target_pairs={{0,1},{1,2},{2,3},{3,4},{4,5},{5,6},{6,7},{7,8},{8,9},{9,10},{10,1... | collective-permute-start | bytes 196616 | tf_op jit(solution)/shard_map/while/body/eval_jaxpr/ppermute | solution.py:12
  171.3 5.6 %collective-permute-start = (f32[32,512]{1,0:T(8,128)S(1)}, f32[32,512]{1,0:T(8,128)S(1)}, u32[]{:S(2)}, u32[]{:S(2)}) collective-permute-start(f32[32,512]{1,0:T(8,128)S(1)} %convolution_add_fusion.10), channel_id=1, source_target_pairs={{0,1},{1,2},{2,3},{3,4},{4,5},{5,6},{6,7},{7,8},{8,9},{9,10},{10,1... | collective-permute-start | bytes 196616 | tf_op jit(solution)/shard_map/while/body/eval_jaxpr/ppermute | solution.py:12
  179.8 5.6 %collective-permute-start = (f32[32,512]{1,0:T(8,128)S(1)}, f32[32,512]{1,0:T(8,128)S(1)}, u32[]{:S(2)}, u32[]{:S(2)}) collective-permute-start(f32[32,512]{1,0:T(8,128)S(1)} %convolution_add_fusion.10), channel_id=1, source_target_pairs={{0,1},{1,2},{2,3},{3,4},{4,5},{5,6},{6,7},{7,8},{8,9},{9,10},{10,1... | collective-permute-start | bytes 196616 | tf_op jit(solution)/shard_map/while/body/eval_jaxpr/ppermute | solution.py:12
  188.2 5.6 %collective-permute-start = (f32[32,512]{1,0:T(8,128)S(1)}, f32[32,512]{1,0:T(8,128)S(1)}, u32[]{:S(2)}, u32[]{:S(2)}) collective-permute-start(f32[32,512]{1,0:T(8,128)S(1)} %convolution_add_fusion.10), channel_id=1, source_target_pairs={{0,1},{1,2},{2,3},{3,4},{4,5},{5,6},{6,7},{7,8},{8,9},{9,10},{10,1... | collective-permute-start | bytes 196616 | tf_op jit(solution)/shard_map/while/body/eval_jaxpr/ppermute | solution.py:12
  196.7 5.6 %collective-permute-start = (f32[32,512]{1,0:T(8,128)S(1)}, f32[32,512]{1,0:T(8,128)S(1)}, u32[]{:S(2)}, u32[]{:S(2)}) collective-permute-start(f32[32,512]{1,0:T(8,128)S(1)} %convolution_add_fusion.10), channel_id=1, source_target_pairs={{0,1},{1,2},{2,3},{3,4},{4,5},{5,6},{6,7},{7,8},{8,9},{9,10},{10,1... | collective-permute-start | bytes 196616 | tf_op jit(solution)/shard_map/while/body/eval_jaxpr/ppermute | solution.py:12
  205.1 5.6 %collective-permute-start = (f32[32,512]{1,0:T(8,128)S(1)}, f32[32,512]{1,0:T(8,128)S(1)}, u32[]{:S(2)}, u32[]{:S(2)}) collective-permute-start(f32[32,512]{1,0:T(8,128)S(1)} %convolution_add_fusion.10), channel_id=1, source_target_pairs={{0,1},{1,2},{2,3},{3,4},{4,5},{5,6},{6,7},{7,8},{8,9},{9,10},{10,1... | collective-permute-start | bytes 196616 | tf_op jit(solution)/shard_map/while/body/eval_jaxpr/ppermute | solution.py:12
  213.6 5.6 %collective-permute-start = (f32[32,512]{1,0:T(8,128)S(1)}, f32[32,512]{1,0:T(8,128)S(1)}, u32[]{:S(2)}, u32[]{:S(2)}) collective-permute-start(f32[32,512]{1,0:T(8,128)S(1)} %convolution_add_fusion.10), channel_id=1, source_target_pairs={{0,1},{1,2},{2,3},{3,4},{4,5},{5,6},{6,7},{7,8},{8,9},{9,10},{10,1... | collective-permute-start | bytes 196616 | tf_op jit(solution)/shard_map/while/body/eval_jaxpr/ppermute | solution.py:12
  222.1 5.6 %collective-permute-start = (f32[32,512]{1,0:T(8,128)S(1)}, f32[32,512]{1,0:T(8,128)S(1)}, u32[]{:S(2)}, u32[]{:S(2)}) collective-permute-start(f32[32,512]{1,0:T(8,128)S(1)} %convolution_add_fusion.10), channel_id=1, source_target_pairs={{0,1},{1,2},{2,3},{3,4},{4,5},{5,6},{6,7},{7,8},{8,9},{9,10},{10,1... | collective-permute-start | bytes 196616 | tf_op jit(solution)/shard_map/while/body/eval_jaxpr/ppermute | solution.py:12
  228.6 18.7 %while.106 = (s32[]{:T(128)}, f32[4,2,32,256]{3,2,1,0:T(8,128)S(1)}, f32[2,4,2,32,256]{4,3,1,2,0:T(8,128)S(1)}, s32[2]{0:T(128)S(1)}, f32[2,32,256]{2,1,0:T(8,12...) while((s32[]{:T(128)}, f32[4,2,32,256]{3,2,1,0:T(8,128)S(1)}, ...), condition=%wide.region_8.9_spmd, body=%wide.region_7.8_spmd.sunk | while | flops 604241920 | bytes 11141283 | solution.py:57
  247.3 18.4 %while.109 = (s32[]{:T(128)}, f32[4,2,32,256]{3,2,0,1:T(8,128)S(1)}, s32[2]{0:T(128)S(1)}, f32[2,256,256]{2,1,0:T(8,128)S(1)}, f32[4,2,2,256,256]{4,3,0,2,1:T(8,...) while((s32[]{:T(128)}, f32[4,2,32,256]{3,2,0,1:T(8,128)S(1)}, ...), condition=%wide.region_10.11_spmd.clone, body=%wide.region_9.10_spmd.clone.sunk | while | flops 604241920 | bytes 11272365 | solution.py:72
  265.8 4.5 maximum_maximum_fusion
  270.3 153.2 %while.107 = (s32[]{:T(128)}, f32[4,32,512]{2,1,0:T(8,128)S(1)}, s32[]{:T(128)}, f32[4,512,512]{2,1,0:T(8,128)}, f32[4,32,512]{2,1,0:T(8,128)S(1)}, /*index=5*/s32[]{:T(128)}, s32[]{:T(128)}, s32[]{:T(128)}, s32[]{:T(128)}) while((s32[]{:T(128)}, f32[4,32,512]{2,1,0:T(8,128)S(1)}, s32[]{:T(128)}, f32[4,512,512]{2,1,0:T(8,128)}, ...), condition=%wide.region_12.13_spmd, body=%wide.region_11.12_spmd.sunk | while | flops 100696072 | bytes 1836779 | solution.py:108
  273.6 5.0 %collective-permute-done.1 = f32[32,512]{1,0:T(8,128)S(1)} collective-permute-done((f32[32,512]{1,0:T(8,128)S(1)}, f32[32,512]{1,0:T(8,128)S(1)}, u32[]{:S(2)}, u32[]{:S(2)}) %collective-permute-start.1) | collective-permute-done | bytes 65568 | tf_op jit(solution)/shard_map/while/body/eval_jaxpr/ppermute | solution.py:12
  281.9 5.8 %collective-permute-done.1 = f32[32,512]{1,0:T(8,128)S(1)} collective-permute-done((f32[32,512]{1,0:T(8,128)S(1)}, f32[32,512]{1,0:T(8,128)S(1)}, u32[]{:S(2)}, u32[]{:S(2)}) %collective-permute-start.1) | collective-permute-done | bytes 65568 | tf_op jit(solution)/shard_map/while/body/eval_jaxpr/ppermute | solution.py:12
  291.0 5.0 %collective-permute-done.1 = f32[32,512]{1,0:T(8,128)S(1)} collective-permute-done((f32[32,512]{1,0:T(8,128)S(1)}, f32[32,512]{1,0:T(8,128)S(1)}, u32[]{:S(2)}, u32[]{:S(2)}) %collective-permute-start.1) | collective-permute-done | bytes 65568 | tf_op jit(solution)/shard_map/while/body/eval_jaxpr/ppermute | solution.py:12
  299.3 5.8 %collective-permute-done.1 = f32[32,512]{1,0:T(8,128)S(1)} collective-permute-done((f32[32,512]{1,0:T(8,128)S(1)}, f32[32,512]{1,0:T(8,128)S(1)}, u32[]{:S(2)}, u32[]{:S(2)}) %collective-permute-start.1) | collective-permute-done | bytes 65568 | tf_op jit(solution)/shard_map/while/body/eval_jaxpr/ppermute | solution.py:12
  308.4 5.1 %collective-permute-done.1 = f32[32,512]{1,0:T(8,128)S(1)} collective-permute-done((f32[32,512]{1,0:T(8,128)S(1)}, f32[32,512]{1,0:T(8,128)S(1)}, u32[]{:S(2)}, u32[]{:S(2)}) %collective-permute-start.1) | collective-permute-done | bytes 65568 | tf_op jit(solution)/shard_map/while/body/eval_jaxpr/ppermute | solution.py:12
  316.9 5.1 %collective-permute-done.1 = f32[32,512]{1,0:T(8,128)S(1)} collective-permute-done((f32[32,512]{1,0:T(8,128)S(1)}, f32[32,512]{1,0:T(8,128)S(1)}, u32[]{:S(2)}, u32[]{:S(2)}) %collective-permute-start.1) | collective-permute-done | bytes 65568 | tf_op jit(solution)/shard_map/while/body/eval_jaxpr/ppermute | solution.py:12
  325.3 5.1 %collective-permute-done.1 = f32[32,512]{1,0:T(8,128)S(1)} collective-permute-done((f32[32,512]{1,0:T(8,128)S(1)}, f32[32,512]{1,0:T(8,128)S(1)}, u32[]{:S(2)}, u32[]{:S(2)}) %collective-permute-start.1) | collective-permute-done | bytes 65568 | tf_op jit(solution)/shard_map/while/body/eval_jaxpr/ppermute | solution.py:12
  333.8 5.1 %collective-permute-done.1 = f32[32,512]{1,0:T(8,128)S(1)} collective-permute-done((f32[32,512]{1,0:T(8,128)S(1)}, f32[32,512]{1,0:T(8,128)S(1)}, u32[]{:S(2)}, u32[]{:S(2)}) %collective-permute-start.1) | collective-permute-done | bytes 65568 | tf_op jit(solution)/shard_map/while/body/eval_jaxpr/ppermute | solution.py:12
  342.3 5.1 %collective-permute-done.1 = f32[32,512]{1,0:T(8,128)S(1)} collective-permute-done((f32[32,512]{1,0:T(8,128)S(1)}, f32[32,512]{1,0:T(8,128)S(1)}, u32[]{:S(2)}, u32[]{:S(2)}) %collective-permute-start.1) | collective-permute-done | bytes 65568 | tf_op jit(solution)/shard_map/while/body/eval_jaxpr/ppermute | solution.py:12
  350.7 5.1 %collective-permute-done.1 = f32[32,512]{1,0:T(8,128)S(1)} collective-permute-done((f32[32,512]{1,0:T(8,128)S(1)}, f32[32,512]{1,0:T(8,128)S(1)}, u32[]{:S(2)}, u32[]{:S(2)}) %collective-permute-start.1) | collective-permute-done | bytes 65568 | tf_op jit(solution)/shard_map/while/body/eval_jaxpr/ppermute | solution.py:12
  359.2 5.1 %collective-permute-done.1 = f32[32,512]{1,0:T(8,128)S(1)} collective-permute-done((f32[32,512]{1,0:T(8,128)S(1)}, f32[32,512]{1,0:T(8,128)S(1)}, u32[]{:S(2)}, u32[]{:S(2)}) %collective-permute-start.1) | collective-permute-done | bytes 65568 | tf_op jit(solution)/shard_map/while/body/eval_jaxpr/ppermute | solution.py:12
  367.6 5.1 %collective-permute-done.1 = f32[32,512]{1,0:T(8,128)S(1)} collective-permute-done((f32[32,512]{1,0:T(8,128)S(1)}, f32[32,512]{1,0:T(8,128)S(1)}, u32[]{:S(2)}, u32[]{:S(2)}) %collective-permute-start.1) | collective-permute-done | bytes 65568 | tf_op jit(solution)/shard_map/while/body/eval_jaxpr/ppermute | solution.py:12
  376.1 5.1 %collective-permute-done.1 = f32[32,512]{1,0:T(8,128)S(1)} collective-permute-done((f32[32,512]{1,0:T(8,128)S(1)}, f32[32,512]{1,0:T(8,128)S(1)}, u32[]{:S(2)}, u32[]{:S(2)}) %collective-permute-start.1) | collective-permute-done | bytes 65568 | tf_op jit(solution)/shard_map/while/body/eval_jaxpr/ppermute | solution.py:12
  384.6 5.1 %collective-permute-done.1 = f32[32,512]{1,0:T(8,128)S(1)} collective-permute-done((f32[32,512]{1,0:T(8,128)S(1)}, f32[32,512]{1,0:T(8,128)S(1)}, u32[]{:S(2)}, u32[]{:S(2)}) %collective-permute-start.1) | collective-permute-done | bytes 65568 | tf_op jit(solution)/shard_map/while/body/eval_jaxpr/ppermute | solution.py:12
  393.0 5.1 %collective-permute-done.1 = f32[32,512]{1,0:T(8,128)S(1)} collective-permute-done((f32[32,512]{1,0:T(8,128)S(1)}, f32[32,512]{1,0:T(8,128)S(1)}, u32[]{:S(2)}, u32[]{:S(2)}) %collective-permute-start.1) | collective-permute-done | bytes 65568 | tf_op jit(solution)/shard_map/while/body/eval_jaxpr/ppermute | solution.py:12
  401.5 5.1 %collective-permute-done.1 = f32[32,512]{1,0:T(8,128)S(1)} collective-permute-done((f32[32,512]{1,0:T(8,128)S(1)}, f32[32,512]{1,0:T(8,128)S(1)}, u32[]{:S(2)}, u32[]{:S(2)}) %collective-permute-start.1) | collective-permute-done | bytes 65568 | tf_op jit(solution)/shard_map/while/body/eval_jaxpr/ppermute | solution.py:12
  409.9 5.1 %collective-permute-done.1 = f32[32,512]{1,0:T(8,128)S(1)} collective-permute-done((f32[32,512]{1,0:T(8,128)S(1)}, f32[32,512]{1,0:T(8,128)S(1)}, u32[]{:S(2)}, u32[]{:S(2)}) %collective-permute-start.1) | collective-permute-done | bytes 65568 | tf_op jit(solution)/shard_map/while/body/eval_jaxpr/ppermute | solution.py:12
  418.4 5.1 %collective-permute-done.1 = f32[32,512]{1,0:T(8,128)S(1)} collective-permute-done((f32[32,512]{1,0:T(8,128)S(1)}, f32[32,512]{1,0:T(8,128)S(1)}, u32[]{:S(2)}, u32[]{:S(2)}) %collective-permute-start.1) | collective-permute-done | bytes 65568 | tf_op jit(solution)/shard_map/while/body/eval_jaxpr/ppermute | solution.py:12
  423.7 18.7 %while.108 = (s32[]{:T(128)}, f32[4,2,32,256]{3,2,0,1:T(8,128)S(1)}, f32[2,4,2,32,256]{4,1,2,3,0:T(4,128)S(1)}, s32[2]{0:T(128)S(1)}, f32[2,256,256]{2,1,0:T(8,1...) while((s32[]{:T(128)}, f32[4,2,32,256]{3,2,0,1:T(8,128)S(1)}, ...), condition=%wide.region_14.15_spmd, body=%wide.region_13.14_spmd.sunk | while | flops 604307456 | bytes 12583091 | solution.py:72
  445.0 6.4 %collective-permute-start.3 = (f32[32,256]{1,0:T(8,128)S(1)}, f32[32,256]{1,0:T(8,128)S(1)}, u32[]{:S(2)}, u32[]{:S(2)}) collective-permute-start(f32[32,256]{1,0:T(8,128)S(1)} %get-tuple-element.982), channel_id=1, source_target_pairs={{0,1},{1,2},{2,3},{3,4},{4,5},{5,6},{6,7},{7,8},{8,9},{9,10},{10,1... | collective-permute-start | bytes 98312 | tf_op jit(solution)/shard_map/ppermute | solution.py:12
  456.7 6.3 %collective-permute-start.5 = (f32[2,32,32]{2,1,0:T(8,128)S(1)}, f32[2,32,32]{2,1,0:T(8,128)S(1)}, u32[]{:S(2)}, u32[]{:S(2)}) collective-permute-start(f32[2,32,32]{2,1,0:T(8,128)S(1)} %fusion.65), channel_id=1, source_target_pairs={{0,2},{1,3},{2,0},{3,1},{4,6},{5,7},{6,4},{7,5},{8,10},{9,11},{10,... | collective-permute-start | bytes 24584 | tf_op jit(solution)/shard_map/ppermute | solution.py:21
  465.0 4.1 collective-permute-start.6
  (328 shorter events, 238.1 us)
Async XLA Ops:
  0.6 450.7 %copy-start = (f32[2,256,256]{2,1,0:T(8,128)S(1)}, f32[2,256,256]{2,1,0:T(8,128)}, u32[]{:S(2)}) copy-start(f32[2,256,256]{2,1,0:T(8,128)} %param.35) | copy-start | bytes 1572868
  0.7 4.7 copy-start.8
  85.4 143.2 %copy-start.3 = (f32[2,4,2,32,256]{4,3,1,2,0:T(8,128)S(1)}, f32[2,4,2,32,256]{4,3,1,2,0:T(8,128)}, u32[]{:S(2)}) copy-start(f32[2,4,2,32,256]{4,3,1,2,0:T(8,128)} %custom-call.1) | copy-start | bytes 1572868
  87.4 3.3 collective-permute-start
  92.7 5.8 %collective-permute-start = (f32[32,512]{1,0:T(8,128)S(1)}, f32[32,512]{1,0:T(8,128)S(1)}, u32[]{:S(2)}, u32[]{:S(2)}) collective-permute-start(f32[32,512]{1,0:T(8,128)S(1)} %convolution_add_fusion.10), channel_id=1, source_target_pairs={{0,1},{1,2},{2,3},{3,4},{4,5},{5,6},{6,7},{7,8},{8,9},{9,10},{10,1... | collective-permute-start | bytes 196616 | tf_op jit(solution)/shard_map/while/body/eval_jaxpr/ppermute | solution.py:12
  100.5 5.6 %collective-permute-start = (f32[32,512]{1,0:T(8,128)S(1)}, f32[32,512]{1,0:T(8,128)S(1)}, u32[]{:S(2)}, u32[]{:S(2)}) collective-permute-start(f32[32,512]{1,0:T(8,128)S(1)} %convolution_add_fusion.10), channel_id=1, source_target_pairs={{0,1},{1,2},{2,3},{3,4},{4,5},{5,6},{6,7},{7,8},{8,9},{9,10},{10,1... | collective-permute-start | bytes 196616 | tf_op jit(solution)/shard_map/while/body/eval_jaxpr/ppermute | solution.py:12
  108.0 5.6 %collective-permute-start = (f32[32,512]{1,0:T(8,128)S(1)}, f32[32,512]{1,0:T(8,128)S(1)}, u32[]{:S(2)}, u32[]{:S(2)}) collective-permute-start(f32[32,512]{1,0:T(8,128)S(1)} %convolution_add_fusion.10), channel_id=1, source_target_pairs={{0,1},{1,2},{2,3},{3,4},{4,5},{5,6},{6,7},{7,8},{8,9},{9,10},{10,1... | collective-permute-start | bytes 196616 | tf_op jit(solution)/shard_map/while/body/eval_jaxpr/ppermute | solution.py:12
  115.6 5.6 %collective-permute-start = (f32[32,512]{1,0:T(8,128)S(1)}, f32[32,512]{1,0:T(8,128)S(1)}, u32[]{:S(2)}, u32[]{:S(2)}) collective-permute-start(f32[32,512]{1,0:T(8,128)S(1)} %convolution_add_fusion.10), channel_id=1, source_target_pairs={{0,1},{1,2},{2,3},{3,4},{4,5},{5,6},{6,7},{7,8},{8,9},{9,10},{10,1... | collective-permute-start | bytes 196616 | tf_op jit(solution)/shard_map/while/body/eval_jaxpr/ppermute | solution.py:12
  123.2 5.6 %collective-permute-start = (f32[32,512]{1,0:T(8,128)S(1)}, f32[32,512]{1,0:T(8,128)S(1)}, u32[]{:S(2)}, u32[]{:S(2)}) collective-permute-start(f32[32,512]{1,0:T(8,128)S(1)} %convolution_add_fusion.10), channel_id=1, source_target_pairs={{0,1},{1,2},{2,3},{3,4},{4,5},{5,6},{6,7},{7,8},{8,9},{9,10},{10,1... | collective-permute-start | bytes 196616 | tf_op jit(solution)/shard_map/while/body/eval_jaxpr/ppermute | solution.py:12
  130.7 5.6 %collective-permute-start = (f32[32,512]{1,0:T(8,128)S(1)}, f32[32,512]{1,0:T(8,128)S(1)}, u32[]{:S(2)}, u32[]{:S(2)}) collective-permute-start(f32[32,512]{1,0:T(8,128)S(1)} %convolution_add_fusion.10), channel_id=1, source_target_pairs={{0,1},{1,2},{2,3},{3,4},{4,5},{5,6},{6,7},{7,8},{8,9},{9,10},{10,1... | collective-permute-start | bytes 196616 | tf_op jit(solution)/shard_map/while/body/eval_jaxpr/ppermute | solution.py:12
  138.3 5.7 %collective-permute-start = (f32[32,512]{1,0:T(8,128)S(1)}, f32[32,512]{1,0:T(8,128)S(1)}, u32[]{:S(2)}, u32[]{:S(2)}) collective-permute-start(f32[32,512]{1,0:T(8,128)S(1)} %convolution_add_fusion.10), channel_id=1, source_target_pairs={{0,1},{1,2},{2,3},{3,4},{4,5},{5,6},{6,7},{7,8},{8,9},{9,10},{10,1... | collective-permute-start | bytes 196616 | tf_op jit(solution)/shard_map/while/body/eval_jaxpr/ppermute | solution.py:12
  145.9 6.5 %collective-permute-start = (f32[32,512]{1,0:T(8,128)S(1)}, f32[32,512]{1,0:T(8,128)S(1)}, u32[]{:S(2)}, u32[]{:S(2)}) collective-permute-start(f32[32,512]{1,0:T(8,128)S(1)} %convolution_add_fusion.10), channel_id=1, source_target_pairs={{0,1},{1,2},{2,3},{3,4},{4,5},{5,6},{6,7},{7,8},{8,9},{9,10},{10,1... | collective-permute-start | bytes 196616 | tf_op jit(solution)/shard_map/while/body/eval_jaxpr/ppermute | solution.py:12
  154.4 6.5 %collective-permute-start = (f32[32,512]{1,0:T(8,128)S(1)}, f32[32,512]{1,0:T(8,128)S(1)}, u32[]{:S(2)}, u32[]{:S(2)}) collective-permute-start(f32[32,512]{1,0:T(8,128)S(1)} %convolution_add_fusion.10), channel_id=1, source_target_pairs={{0,1},{1,2},{2,3},{3,4},{4,5},{5,6},{6,7},{7,8},{8,9},{9,10},{10,1... | collective-permute-start | bytes 196616 | tf_op jit(solution)/shard_map/while/body/eval_jaxpr/ppermute | solution.py:12
  162.8 6.5 %collective-permute-start = (f32[32,512]{1,0:T(8,128)S(1)}, f32[32,512]{1,0:T(8,128)S(1)}, u32[]{:S(2)}, u32[]{:S(2)}) collective-permute-start(f32[32,512]{1,0:T(8,128)S(1)} %convolution_add_fusion.10), channel_id=1, source_target_pairs={{0,1},{1,2},{2,3},{3,4},{4,5},{5,6},{6,7},{7,8},{8,9},{9,10},{10,1... | collective-permute-start | bytes 196616 | tf_op jit(solution)/shard_map/while/body/eval_jaxpr/ppermute | solution.py:12
  171.3 6.5 %collective-permute-start = (f32[32,512]{1,0:T(8,128)S(1)}, f32[32,512]{1,0:T(8,128)S(1)}, u32[]{:S(2)}, u32[]{:S(2)}) collective-permute-start(f32[32,512]{1,0:T(8,128)S(1)} %convolution_add_fusion.10), channel_id=1, source_target_pairs={{0,1},{1,2},{2,3},{3,4},{4,5},{5,6},{6,7},{7,8},{8,9},{9,10},{10,1... | collective-permute-start | bytes 196616 | tf_op jit(solution)/shard_map/while/body/eval_jaxpr/ppermute | solution.py:12
  179.8 6.5 %collective-permute-start = (f32[32,512]{1,0:T(8,128)S(1)}, f32[32,512]{1,0:T(8,128)S(1)}, u32[]{:S(2)}, u32[]{:S(2)}) collective-permute-start(f32[32,512]{1,0:T(8,128)S(1)} %convolution_add_fusion.10), channel_id=1, source_target_pairs={{0,1},{1,2},{2,3},{3,4},{4,5},{5,6},{6,7},{7,8},{8,9},{9,10},{10,1... | collective-permute-start | bytes 196616 | tf_op jit(solution)/shard_map/while/body/eval_jaxpr/ppermute | solution.py:12
  188.2 6.5 %collective-permute-start = (f32[32,512]{1,0:T(8,128)S(1)}, f32[32,512]{1,0:T(8,128)S(1)}, u32[]{:S(2)}, u32[]{:S(2)}) collective-permute-start(f32[32,512]{1,0:T(8,128)S(1)} %convolution_add_fusion.10), channel_id=1, source_target_pairs={{0,1},{1,2},{2,3},{3,4},{4,5},{5,6},{6,7},{7,8},{8,9},{9,10},{10,1... | collective-permute-start | bytes 196616 | tf_op jit(solution)/shard_map/while/body/eval_jaxpr/ppermute | solution.py:12
  196.7 6.5 %collective-permute-start = (f32[32,512]{1,0:T(8,128)S(1)}, f32[32,512]{1,0:T(8,128)S(1)}, u32[]{:S(2)}, u32[]{:S(2)}) collective-permute-start(f32[32,512]{1,0:T(8,128)S(1)} %convolution_add_fusion.10), channel_id=1, source_target_pairs={{0,1},{1,2},{2,3},{3,4},{4,5},{5,6},{6,7},{7,8},{8,9},{9,10},{10,1... | collective-permute-start | bytes 196616 | tf_op jit(solution)/shard_map/while/body/eval_jaxpr/ppermute | solution.py:12
  205.1 6.5 %collective-permute-start = (f32[32,512]{1,0:T(8,128)S(1)}, f32[32,512]{1,0:T(8,128)S(1)}, u32[]{:S(2)}, u32[]{:S(2)}) collective-permute-start(f32[32,512]{1,0:T(8,128)S(1)} %convolution_add_fusion.10), channel_id=1, source_target_pairs={{0,1},{1,2},{2,3},{3,4},{4,5},{5,6},{6,7},{7,8},{8,9},{9,10},{10,1... | collective-permute-start | bytes 196616 | tf_op jit(solution)/shard_map/while/body/eval_jaxpr/ppermute | solution.py:12
  213.6 6.5 %collective-permute-start = (f32[32,512]{1,0:T(8,128)S(1)}, f32[32,512]{1,0:T(8,128)S(1)}, u32[]{:S(2)}, u32[]{:S(2)}) collective-permute-start(f32[32,512]{1,0:T(8,128)S(1)} %convolution_add_fusion.10), channel_id=1, source_target_pairs={{0,1},{1,2},{2,3},{3,4},{4,5},{5,6},{6,7},{7,8},{8,9},{9,10},{10,1... | collective-permute-start | bytes 196616 | tf_op jit(solution)/shard_map/while/body/eval_jaxpr/ppermute | solution.py:12
  222.1 6.5 %collective-permute-start = (f32[32,512]{1,0:T(8,128)S(1)}, f32[32,512]{1,0:T(8,128)S(1)}, u32[]{:S(2)}, u32[]{:S(2)}) collective-permute-start(f32[32,512]{1,0:T(8,128)S(1)} %convolution_add_fusion.10), channel_id=1, source_target_pairs={{0,1},{1,2},{2,3},{3,4},{4,5},{5,6},{6,7},{7,8},{8,9},{9,10},{10,1... | collective-permute-start | bytes 196616 | tf_op jit(solution)/shard_map/while/body/eval_jaxpr/ppermute | solution.py:12
  247.3 18.5 %copy-start.5 = (f32[4,256,256]{2,1,0:T(8,128)S(1)}, f32[4,256,256]{2,1,0:T(8,128)}, u32[]{:S(2)}) copy-start(f32[4,256,256]{2,1,0:T(8,128)} %fusion.68) | copy-start | bytes 3145732
  272.3 6.3 %collective-permute-start.1 = (f32[32,512]{1,0:T(8,128)S(1)}, f32[32,512]{1,0:T(8,128)S(1)}, u32[]{:S(2)}, u32[]{:S(2)}) collective-permute-start(f32[32,512]{1,0:T(8,128)S(1)} %convolution_add_fusion.11), channel_id=1, source_target_pairs={{1,0},{2,1},{3,2},{4,3},{5,4},{6,5},{7,6},{8,7},{9,8},{10,9},{11,1... | collective-permute-start | bytes 196616 | tf_op jit(solution)/shard_map/while/body/eval_jaxpr/ppermute | solution.py:12
  280.6 7.1 %collective-permute-start.1 = (f32[32,512]{1,0:T(8,128)S(1)}, f32[32,512]{1,0:T(8,128)S(1)}, u32[]{:S(2)}, u32[]{:S(2)}) collective-permute-start(f32[32,512]{1,0:T(8,128)S(1)} %convolution_add_fusion.11), channel_id=1, source_target_pairs={{1,0},{2,1},{3,2},{4,3},{5,4},{6,5},{7,6},{8,7},{9,8},{10,9},{11,1... | collective-permute-start | bytes 196616 | tf_op jit(solution)/shard_map/while/body/eval_jaxpr/ppermute | solution.py:12
  289.7 6.3 %collective-permute-start.1 = (f32[32,512]{1,0:T(8,128)S(1)}, f32[32,512]{1,0:T(8,128)S(1)}, u32[]{:S(2)}, u32[]{:S(2)}) collective-permute-start(f32[32,512]{1,0:T(8,128)S(1)} %convolution_add_fusion.11), channel_id=1, source_target_pairs={{1,0},{2,1},{3,2},{4,3},{5,4},{6,5},{7,6},{8,7},{9,8},{10,9},{11,1... | collective-permute-start | bytes 196616 | tf_op jit(solution)/shard_map/while/body/eval_jaxpr/ppermute | solution.py:12
  298.0 7.1 %collective-permute-start.1 = (f32[32,512]{1,0:T(8,128)S(1)}, f32[32,512]{1,0:T(8,128)S(1)}, u32[]{:S(2)}, u32[]{:S(2)}) collective-permute-start(f32[32,512]{1,0:T(8,128)S(1)} %convolution_add_fusion.11), channel_id=1, source_target_pairs={{1,0},{2,1},{3,2},{4,3},{5,4},{6,5},{7,6},{8,7},{9,8},{10,9},{11,1... | collective-permute-start | bytes 196616 | tf_op jit(solution)/shard_map/while/body/eval_jaxpr/ppermute | solution.py:12
  307.1 6.5 %collective-permute-start.1 = (f32[32,512]{1,0:T(8,128)S(1)}, f32[32,512]{1,0:T(8,128)S(1)}, u32[]{:S(2)}, u32[]{:S(2)}) collective-permute-start(f32[32,512]{1,0:T(8,128)S(1)} %convolution_add_fusion.11), channel_id=1, source_target_pairs={{1,0},{2,1},{3,2},{4,3},{5,4},{6,5},{7,6},{8,7},{9,8},{10,9},{11,1... | collective-permute-start | bytes 196616 | tf_op jit(solution)/shard_map/while/body/eval_jaxpr/ppermute | solution.py:12
  315.5 6.5 %collective-permute-start.1 = (f32[32,512]{1,0:T(8,128)S(1)}, f32[32,512]{1,0:T(8,128)S(1)}, u32[]{:S(2)}, u32[]{:S(2)}) collective-permute-start(f32[32,512]{1,0:T(8,128)S(1)} %convolution_add_fusion.11), channel_id=1, source_target_pairs={{1,0},{2,1},{3,2},{4,3},{5,4},{6,5},{7,6},{8,7},{9,8},{10,9},{11,1... | collective-permute-start | bytes 196616 | tf_op jit(solution)/shard_map/while/body/eval_jaxpr/ppermute | solution.py:12
  324.0 6.5 %collective-permute-start.1 = (f32[32,512]{1,0:T(8,128)S(1)}, f32[32,512]{1,0:T(8,128)S(1)}, u32[]{:S(2)}, u32[]{:S(2)}) collective-permute-start(f32[32,512]{1,0:T(8,128)S(1)} %convolution_add_fusion.11), channel_id=1, source_target_pairs={{1,0},{2,1},{3,2},{4,3},{5,4},{6,5},{7,6},{8,7},{9,8},{10,9},{11,1... | collective-permute-start | bytes 196616 | tf_op jit(solution)/shard_map/while/body/eval_jaxpr/ppermute | solution.py:12
  332.5 6.5 %collective-permute-start.1 = (f32[32,512]{1,0:T(8,128)S(1)}, f32[32,512]{1,0:T(8,128)S(1)}, u32[]{:S(2)}, u32[]{:S(2)}) collective-permute-start(f32[32,512]{1,0:T(8,128)S(1)} %convolution_add_fusion.11), channel_id=1, source_target_pairs={{1,0},{2,1},{3,2},{4,3},{5,4},{6,5},{7,6},{8,7},{9,8},{10,9},{11,1... | collective-permute-start | bytes 196616 | tf_op jit(solution)/shard_map/while/body/eval_jaxpr/ppermute | solution.py:12
  340.9 6.5 %collective-permute-start.1 = (f32[32,512]{1,0:T(8,128)S(1)}, f32[32,512]{1,0:T(8,128)S(1)}, u32[]{:S(2)}, u32[]{:S(2)}) collective-permute-start(f32[32,512]{1,0:T(8,128)S(1)} %convolution_add_fusion.11), channel_id=1, source_target_pairs={{1,0},{2,1},{3,2},{4,3},{5,4},{6,5},{7,6},{8,7},{9,8},{10,9},{11,1... | collective-permute-start | bytes 196616 | tf_op jit(solution)/shard_map/while/body/eval_jaxpr/ppermute | solution.py:12
  349.4 6.5 %collective-permute-start.1 = (f32[32,512]{1,0:T(8,128)S(1)}, f32[32,512]{1,0:T(8,128)S(1)}, u32[]{:S(2)}, u32[]{:S(2)}) collective-permute-start(f32[32,512]{1,0:T(8,128)S(1)} %convolution_add_fusion.11), channel_id=1, source_target_pairs={{1,0},{2,1},{3,2},{4,3},{5,4},{6,5},{7,6},{8,7},{9,8},{10,9},{11,1... | collective-permute-start | bytes 196616 | tf_op jit(solution)/shard_map/while/body/eval_jaxpr/ppermute | solution.py:12
  357.8 6.5 %collective-permute-start.1 = (f32[32,512]{1,0:T(8,128)S(1)}, f32[32,512]{1,0:T(8,128)S(1)}, u32[]{:S(2)}, u32[]{:S(2)}) collective-permute-start(f32[32,512]{1,0:T(8,128)S(1)} %convolution_add_fusion.11), channel_id=1, source_target_pairs={{1,0},{2,1},{3,2},{4,3},{5,4},{6,5},{7,6},{8,7},{9,8},{10,9},{11,1... | collective-permute-start | bytes 196616 | tf_op jit(solution)/shard_map/while/body/eval_jaxpr/ppermute | solution.py:12
  366.3 6.5 %collective-permute-start.1 = (f32[32,512]{1,0:T(8,128)S(1)}, f32[32,512]{1,0:T(8,128)S(1)}, u32[]{:S(2)}, u32[]{:S(2)}) collective-permute-start(f32[32,512]{1,0:T(8,128)S(1)} %convolution_add_fusion.11), channel_id=1, source_target_pairs={{1,0},{2,1},{3,2},{4,3},{5,4},{6,5},{7,6},{8,7},{9,8},{10,9},{11,1... | collective-permute-start | bytes 196616 | tf_op jit(solution)/shard_map/while/body/eval_jaxpr/ppermute | solution.py:12
  374.8 6.5 %collective-permute-start.1 = (f32[32,512]{1,0:T(8,128)S(1)}, f32[32,512]{1,0:T(8,128)S(1)}, u32[]{:S(2)}, u32[]{:S(2)}) collective-permute-start(f32[32,512]{1,0:T(8,128)S(1)} %convolution_add_fusion.11), channel_id=1, source_target_pairs={{1,0},{2,1},{3,2},{4,3},{5,4},{6,5},{7,6},{8,7},{9,8},{10,9},{11,1... | collective-permute-start | bytes 196616 | tf_op jit(solution)/shard_map/while/body/eval_jaxpr/ppermute | solution.py:12
  383.2 6.5 %collective-permute-start.1 = (f32[32,512]{1,0:T(8,128)S(1)}, f32[32,512]{1,0:T(8,128)S(1)}, u32[]{:S(2)}, u32[]{:S(2)}) collective-permute-start(f32[32,512]{1,0:T(8,128)S(1)} %convolution_add_fusion.11), channel_id=1, source_target_pairs={{1,0},{2,1},{3,2},{4,3},{5,4},{6,5},{7,6},{8,7},{9,8},{10,9},{11,1... | collective-permute-start | bytes 196616 | tf_op jit(solution)/shard_map/while/body/eval_jaxpr/ppermute | solution.py:12
  391.7 6.5 %collective-permute-start.1 = (f32[32,512]{1,0:T(8,128)S(1)}, f32[32,512]{1,0:T(8,128)S(1)}, u32[]{:S(2)}, u32[]{:S(2)}) collective-permute-start(f32[32,512]{1,0:T(8,128)S(1)} %convolution_add_fusion.11), channel_id=1, source_target_pairs={{1,0},{2,1},{3,2},{4,3},{5,4},{6,5},{7,6},{8,7},{9,8},{10,9},{11,1... | collective-permute-start | bytes 196616 | tf_op jit(solution)/shard_map/while/body/eval_jaxpr/ppermute | solution.py:12
  400.1 6.5 %collective-permute-start.1 = (f32[32,512]{1,0:T(8,128)S(1)}, f32[32,512]{1,0:T(8,128)S(1)}, u32[]{:S(2)}, u32[]{:S(2)}) collective-permute-start(f32[32,512]{1,0:T(8,128)S(1)} %convolution_add_fusion.11), channel_id=1, source_target_pairs={{1,0},{2,1},{3,2},{4,3},{5,4},{6,5},{7,6},{8,7},{9,8},{10,9},{11,1... | collective-permute-start | bytes 196616 | tf_op jit(solution)/shard_map/while/body/eval_jaxpr/ppermute | solution.py:12
  408.6 6.5 %collective-permute-start.1 = (f32[32,512]{1,0:T(8,128)S(1)}, f32[32,512]{1,0:T(8,128)S(1)}, u32[]{:S(2)}, u32[]{:S(2)}) collective-permute-start(f32[32,512]{1,0:T(8,128)S(1)} %convolution_add_fusion.11), channel_id=1, source_target_pairs={{1,0},{2,1},{3,2},{4,3},{5,4},{6,5},{7,6},{8,7},{9,8},{10,9},{11,1... | collective-permute-start | bytes 196616 | tf_op jit(solution)/shard_map/while/body/eval_jaxpr/ppermute | solution.py:12
  417.1 6.5 %collective-permute-start.1 = (f32[32,512]{1,0:T(8,128)S(1)}, f32[32,512]{1,0:T(8,128)S(1)}, u32[]{:S(2)}, u32[]{:S(2)}) collective-permute-start(f32[32,512]{1,0:T(8,128)S(1)} %convolution_add_fusion.11), channel_id=1, source_target_pairs={{1,0},{2,1},{3,2},{4,3},{5,4},{6,5},{7,6},{8,7},{9,8},{10,9},{11,1... | collective-permute-start | bytes 196616 | tf_op jit(solution)/shard_map/while/body/eval_jaxpr/ppermute | solution.py:12
  423.7 18.8 %copy-start.10 = (f32[4,2]{0,1:T(2,128)S(1)}, f32[4,2]{0,1:T(2,128)}, u32[]{:S(2)}) copy-start(f32[4,2]{0,1:T(2,128)} %param.36) | copy-start | bytes 100
  423.7 18.8 %copy-start.11 = (f32[2]{0:T(128)S(1)}, f32[2]{0:T(128)}, u32[]{:S(2)}) copy-start(f32[2]{0:T(128)} %constant.424.clone) | copy-start | bytes 28
  443.2 8.9 %collective-permute-start.2 = (f32[32,256]{1,0:T(8,128)S(1)}, f32[32,256]{1,0:T(8,128)S(1)}, u32[]{:S(2)}, u32[]{:S(2)}) collective-permute-start(f32[32,256]{1,0:T(8,128)S(1)} %get-tuple-element.985), channel_id=1, source_target_pairs={{1,0},{2,1},{3,2},{4,3},{5,4},{6,5},{7,6},{8,7},{9,8},{10,9},{11,1... | collective-permute-start | bytes 98312 | tf_op jit(solution)/shard_map/ppermute | solution.py:12
  445.0 7.2 %collective-permute-start.3 = (f32[32,256]{1,0:T(8,128)S(1)}, f32[32,256]{1,0:T(8,128)S(1)}, u32[]{:S(2)}, u32[]{:S(2)}) collective-permute-start(f32[32,256]{1,0:T(8,128)S(1)} %get-tuple-element.982), channel_id=1, source_target_pairs={{0,1},{1,2},{2,3},{3,4},{4,5},{5,6},{6,7},{7,8},{8,9},{9,10},{10,1... | collective-permute-start | bytes 98312 | tf_op jit(solution)/shard_map/ppermute | solution.py:12
  453.0 3.7 collective-permute-start.4
  456.7 8.3 %collective-permute-start.5 = (f32[2,32,32]{2,1,0:T(8,128)S(1)}, f32[2,32,32]{2,1,0:T(8,128)S(1)}, u32[]{:S(2)}, u32[]{:S(2)}) collective-permute-start(f32[2,32,32]{2,1,0:T(8,128)S(1)} %fusion.65), channel_id=1, source_target_pairs={{0,2},{1,3},{2,0},{3,1},{4,6},{5,7},{6,4},{7,5},{8,10},{9,11},{10,... | collective-permute-start | bytes 24584 | tf_op jit(solution)/shard_map/ppermute | solution.py:21
  465.0 6.0 %collective-permute-start.6 = (f32[2,32,32]{2,1,0:T(8,128)S(1)}, f32[2,32,32]{2,1,0:T(8,128)S(1)}, u32[]{:S(2)}, u32[]{:S(2)}) collective-permute-start(f32[2,32,32]{2,1,0:T(8,128)S(1)} %fusion.79), channel_id=1, source_target_pairs={{0,4},{1,5},{2,6},{3,7},{4,0},{5,1},{6,2},{7,3},{8,12},{9,13},{10,... | collective-permute-start | bytes 24584 | tf_op jit(solution)/shard_map/ppermute | solution.py:21
  471.0 4.9 %collective-permute-start.7 = (f32[2,32,32]{2,1,0:T(8,128)S(1)}, f32[2,32,32]{2,1,0:T(8,128)S(1)}, u32[]{:S(2)}, u32[]{:S(2)}) collective-permute-start(f32[2,32,32]{2,1,0:T(8,128)S(1)} %add.307), channel_id=1, source_target_pairs={{0,8},{1,9},{2,10},{3,11},{4,12},{5,13},{6,14},{7,15},{8,0},{9,1},... | collective-permute-start | bytes 24584 | tf_op jit(solution)/shard_map/ppermute | solution.py:21
  (9 other events, 23.0 us)
